TPU v7x, 1024 devices: a whole 8x8x8 slice. The times are simulated.
1024 devices in a mesh: dp: 4 (over z_lo), seq: 256 (over x, z_hi, y, core).
Axes of the slice: x: 8, y: 8, z: 8 (z_hi: 2, z_lo: 4; z = z_hi * 4 + z_lo), core: 2. Of those that a mesh axis runs over, the one named last changes fastest.
Arguments:
- grad_out: bfloat16 [4, 32768, 6144], P('dp', 'seq'), may hold values from -0.00390625 to 0.00390625
- w_out: bfloat16 [128, 6144], P(None, 'dp'), may hold values from -0.078125 to 0.078125
- queries: bfloat16 [4, 32768, 128], P('dp', 'seq'), may hold values from -6 to 6
- keys_in: bfloat16 [4, 32768, 128], P('dp', 'seq'), may hold values from -6 to 6
- values: bfloat16 [4, 32768, 128], P('dp', 'seq'), may hold values from -6 to 6
- log_decay: float32 [4, 2, 32768], P('dp', None, 'seq'), may hold values from -1.2 to 0
- kv_state: bfloat16 [4, 256, 2, 64, 64], P('dp', 'seq'), may hold values from -512 to 512
Outputs:
- grad_q: bfloat16 [4, 32768, 128], P('dp', 'seq')
- grad_k: bfloat16 [4, 32768, 128], P('dp', 'seq')
- grad_v: bfloat16 [4, 32768, 128], P('dp', 'seq')
All inputs are finite; a program needn't handle non-finite values.
Results may differ from a plain program's by a relative error of at most 0.0059.
Values may be sent and summed in bfloat16 or wider, within the bound.
No kernel may reach another device: no remote copies, remote signals or barrier semaphores. Data moves between devices by JAX's collectives and lax.ppermute only.
A program may use at most 64 MiB of HBM per device.

v0:
```python
import jax
import jax.numpy as jnp
from jax import lax
from jax.sharding import PartitionSpec as P


def entering(array, axis, combine, identity):
    size, index = (lax.axis_size(axis), lax.axis_index(axis))
    everything = jax.tree.map(lambda part: lax.all_gather(part, axis), array)
    start = jax.tree.map(
        lambda part, zero: jnp.broadcast_to(jnp.asarray(zero, part.dtype), part.shape),
        array,
        identity,
    )

    def lap(k, before):
        at = size - 1 - k
        reached = at > index
        new = combine(before, jax.tree.map(lambda part: part[at], everything))
        return jax.tree.map(lambda a, b: jnp.where(reached, a, b), new, before)

    return lax.fori_loop(0, size, lap, start)


def merge_states(earlier, later):
    return (earlier[0] * later[0], later[1] + later[0][:, None, None] * earlier[1])


def on_device(grad_out, w_out, queries, keys_in, values, log_decay, kv_state):
    token_rows = grad_out[0]
    length_dev = token_rows.shape[0]
    head_count = log_decay.shape[1]
    head_size = queries.shape[2] // head_count
    projected = lax.dot_general(
        token_rows,
        lax.all_gather(w_out, "dp", axis=1, tiled=True),
        (((1,), (1,)), ((), ())),
        preferred_element_type=jnp.float32,
    )
    grad_attn = projected.astype(jnp.bfloat16).reshape(length_dev, head_count, head_size)
    query_heads = queries[0].reshape(length_dev, head_count, head_size)
    key_heads = keys_in[0].reshape(length_dev, head_count, head_size)
    value_heads = values[0].reshape(length_dev, head_count, head_size)
    cumul = jnp.cumsum(log_decay[0], axis=1)
    block_total = cumul[:, -1]
    growth = jnp.exp(cumul).T[:, :, None]
    scaled_q = (query_heads * growth).astype(jnp.bfloat16)
    block_terms = jnp.einsum(
        "thd,the->hde", scaled_q, grad_attn, preferred_element_type=jnp.float32
    )
    block_decay = jnp.exp(block_total)
    identity = (jnp.ones((head_count,), jnp.float32), jnp.zeros_like(block_terms))
    combined = entering((block_decay, block_terms), "seq", merge_states, identity)
    future_low = combined[1].astype(jnp.bfloat16)
    log_gaps = cumul[:, :, None] - cumul[:, None, :]
    rows_idx = lax.broadcasted_iota(jnp.int32, (length_dev, length_dev), 0)
    cols_idx = lax.broadcasted_iota(jnp.int32, (length_dev, length_dev), 1)
    lower_mask = rows_idx >= cols_idx
    mask_decay = jnp.where(lower_mask, jnp.exp(jnp.where(lower_mask, log_gaps, 0.0)), 0.0)
    weights_p = (
        jnp.einsum("the,she->hts", grad_attn, value_heads, preferred_element_type=jnp.float32)
        * mask_decay
    ).astype(jnp.bfloat16)
    weights_a = (
        jnp.einsum("thd,shd->hts", query_heads, key_heads, preferred_element_type=jnp.float32)
        * mask_decay
    ).astype(jnp.bfloat16)
    saved_state = kv_state[0, 0]
    after = jnp.exp(block_total[:, None] - cumul).T[:, :, None]
    grad_q = jnp.einsum("hts,shd->thd", weights_p, key_heads, preferred_element_type=jnp.float32)
    grad_q = grad_q + growth * jnp.einsum(
        "the,hde->thd", grad_attn, saved_state, preferred_element_type=jnp.float32
    )
    grad_k = jnp.einsum("hts,thd->shd", weights_p, query_heads, preferred_element_type=jnp.float32)
    grad_k = grad_k + after * jnp.einsum(
        "she,hde->shd", value_heads, future_low, preferred_element_type=jnp.float32
    )
    grad_v = jnp.einsum("hts,the->she", weights_a, grad_attn, preferred_element_type=jnp.float32)
    grad_v = grad_v + after * jnp.einsum(
        "shd,hde->she", key_heads, future_low, preferred_element_type=jnp.float32
    )
    out_shape = (1, length_dev, head_count * head_size)
    return (
        grad_q.reshape(out_shape).astype(jnp.bfloat16),
        grad_k.reshape(out_shape).astype(jnp.bfloat16),
        grad_v.reshape(out_shape).astype(jnp.bfloat16),
    )


def solution(mesh):
    return jax.shard_map(
        on_device,
        mesh=mesh,
        in_specs=(
            P("dp", "seq", None),
            P(None, "dp"),
            P("dp", "seq", None),
            P("dp", "seq", None),
            P("dp", "seq", None),
            P("dp", None, "seq"),
            P("dp", "seq", None, None, None),
        ),
        out_specs=(P("dp", "seq", None), P("dp", "seq", None), P("dp", "seq", None)),
        check_vma=False,
    )
```

profile of v0, /device:TPU:1, one launch (start us, length us, event | category | flops | bytes accessed | tf_op | source)
XLA Modules:
  0.0 1132.8 jit_solution(785000071527422354)
XLA Ops:
  8.8 1.0 reduce_window_sum.11
  10.1 60.5 %all-gather.5.cloned.1.call-done = bf16[128,6144]{1,0:T(8,128)(2,1)} async-done(((bf16[128,1536]{1,0:T(8,128)(2,1)}), bf16[128,6144]{1,0:T(8,128)(2,1)}) %all-gather.5.cloned.1.call-update) | async-done | bytes 1572880 | tf_op jit(solution)/shard_map/all_gather | solution.py:36
  70.6 2.0 fusion.16
  73.4 1.3 dynamic-slice
  75.5 802.6 %all-reduce = f32[512]{0:T(512)S(1)} all-reduce(f32[512]{0:T(512)S(1)} %dynamic-update-slice), channel_id=3, replica_groups=mesh['dp'=4,'seq'=256] {'seq'}, use_global_device_ids=true, to_apply=%add | all-reduce | flops 512 | bytes 4096
  879.8 243.8 %while.16 = (s32[]{:T(128)}, f32[2,64,64]{2,1,0:T(8,128)S(1)}, s32[]{:T(128)}, f32[256,2,64,64]{3,2,1,0:T(8,128)}, f32[256,2]{1,0:T(8,128)S(1)}, /*index=5*/s32[]{:T(128)}, s32[]{:T(128)}, s32[]{:T(128)}, s32[]{:T(128)}) while((s32[]{:T(128)}, f32[2,64,64]{2,1,0:T(8,128)S(1)}, s32[]{:T(128)}, f32[256,2,64,64]{3,2,1,0:T(8,128)}, ...), condition=%wide.region_2.3_spmd.clone, body=%wide.region_1.2_spmd.clone.sunk | while | flops 32776 | bytes 98495 | solution.py:22
  880.8 0.9 fusion.44
  882.7 0.9 fusion.44
  884.6 0.9 fusion.44
  886.5 0.9 fusion.44
  887.5 0.9 fusion.44
  889.4 0.9 fusion.44
  891.3 0.9 fusion.44
  893.2 0.9 fusion.44
  894.1 0.9 fusion.44
  896.0 0.9 fusion.44
  897.9 0.9 fusion.44
  898.9 0.9 fusion.44
  900.8 0.9 fusion.44
  902.7 0.9 fusion.44
  904.6 0.9 fusion.44
  905.6 0.9 fusion.44
  907.5 0.9 fusion.44
  909.4 0.9 fusion.44
  911.3 0.9 fusion.44
  912.2 0.9 fusion.44
  914.1 0.9 fusion.44
  916.0 0.9 fusion.44
  917.0 0.9 fusion.44
  918.9 0.9 fusion.44
  920.8 0.9 fusion.44
  922.7 0.9 fusion.44
  923.7 0.9 fusion.44
  925.6 0.9 fusion.44
  927.5 0.9 fusion.44
  929.4 0.9 fusion.44
  930.3 0.9 fusion.44
  932.2 0.9 fusion.44
  934.1 0.9 fusion.44
  935.1 0.9 fusion.44
  937.0 0.9 fusion.44
  938.9 0.9 fusion.44
  940.8 0.9 fusion.44
  941.8 0.9 fusion.44
  943.7 0.9 fusion.44
  945.6 0.9 fusion.44
  947.5 0.9 fusion.44
  948.4 0.9 fusion.44
  (504 shorter events, 206.8 us)
Async XLA Ops:
  7.2 63.4 %copy-start = (bf16[1,128,6144]{2,1,0:T(8,128)(2,1)S(1)}, bf16[1,128,6144]{2,1,0:T(8,128)(2,1)}, u32[]{:S(2)}) copy-start(bf16[1,128,6144]{2,1,0:T(8,128)(2,1)} %param.9) | copy-start | bytes 4718596
  7.2 63.4 %all-gather.5.cloned.1.call-start = ((), (), s32[]{:S(2)}) async-start(), calls=%async_computation | async-start | bytes 1966080 | tf_op jit(solution)/shard_map/all_gather | solution.py:36
  7.9 871.9 %all-gather.7.cloned.1.call-start = ((), (), s32[]{:S(2)}) async-start(), calls=%async_computation.1 | async-start | bytes 16842752 | tf_op jit(solution)/shard_map/all_gather | solution.py:9
  10.1 868.2 %copy-start.2 = (bf16[1,128,128]{2,1,0:T(8,128)(2,1)S(1)}, bf16[1,128,128]{2,1,0:T(8,128)(2,1)}, u32[]{:S(2)}) copy-start(bf16[1,128,128]{2,1,0:T(8,128)(2,1)} %param.12) | copy-start | bytes 98308
  10.1 868.3 %copy-start.3 = (bf16[1,128,128]{2,1,0:T(8,128)(2,1)S(1)}, bf16[1,128,128]{2,1,0:T(8,128)(2,1)}, u32[]{:S(2)}) copy-start(bf16[1,128,128]{2,1,0:T(8,128)(2,1)} %param.13) | copy-start | bytes 98308
  10.1 868.9 %copy-start.1 = (bf16[1,1,2,64,64]{4,3,2,1,0:T(8,128)(2,1)S(1)}, bf16[1,1,2,64,64]{4,3,2,1,0:T(8,128)(2,1)}, u32[]{:S(2)}) copy-start(bf16[1,1,2,64,64]{4,3,2,1,0:T(8,128)(2,1)} %param.15) | copy-start | bytes 49156
Sparse Core Ops, SparseCore 0:
  10.7 59.8 all-gather.4
  76.4 208.1 all-gather.6
where the time goes:
time: 1150 us; the launch traced here: 1130 us
  blocking collectives  803 us (70%)
  other arithmetic  237 us (21%)
  waiting for transfers between devices  61.2 us (5%)
  between operations  14.8 us (1%)
    unnamed x1, blocking collectives  803 us
    select_n x256, other arithmetic, lap(): return jax.tree.map(lambda a, b: jnp.where(reached, a, b), new, before)  236 us
    all_gather x1, waiting for transfers between devices, on_device(): lax.all_gather(w_out, 'dp', axis=1, tiled=True)  60.5 us
  transfers between devices with their start and end apart: 2, of which 1 were waited for; matrix products, arithmetic and copies ran while one was open for 0% of the time, Pallas kernels for 0%

commit v1 on v0

--- a/solution.py
+++ b/solution.py
@@ -3,27 +3,37 @@
 from jax import lax
 from jax.sharding import PartitionSpec as P
 
+RADIX = 4
 
-def entering(array, axis, combine, identity):
-    size, index = (lax.axis_size(axis), lax.axis_index(axis))
-    everything = jax.tree.map(lambda part: lax.all_gather(part, axis), array)
-    start = jax.tree.map(
-        lambda part, zero: jnp.broadcast_to(jnp.asarray(zero, part.dtype), part.shape),
-        array,
-        identity,
+
+def shifted(array, axis, size, distance):
+    pairs = [(src, src - distance) for src in range(distance, size)]
+    return lax.ppermute(array, axis, pairs)
+
+
+def compose(earlier, later, width):
+    grow = earlier[:, width:width + 1]
+    return jnp.concatenate(
+        [earlier[:, :width] + grow * later[:, :width], earlier[:, width:] * later[:, width:]],
+        axis=1,
     )
 
-    def lap(k, before):
-        at = size - 1 - k
-        reached = at > index
-        new = combine(before, jax.tree.map(lambda part: part[at], everything))
-        return jax.tree.map(lambda a, b: jnp.where(reached, a, b), new, before)
 
-    return lax.fori_loop(0, size, lap, start)
-
-
-def merge_states(earlier, later):
-    return (earlier[0] * later[0], later[1] + later[0][:, None, None] * earlier[1])
+def entering_after(packed, axis, width):
+    size = lax.axis_size(axis)
+    parts = [shifted(packed, axis, size, k) for k in range(1, RADIX + 1)]
+    state = parts[-1]
+    for part in reversed(parts[:-1]):
+        state = compose(part, state, width)
+    span = RADIX
+    while span < size:
+        parts = [shifted(state, axis, size, k * span) for k in range(1, RADIX)]
+        tail = parts[-1]
+        for part in reversed(parts[:-1]):
+            tail = compose(part, tail, width)
+        state = compose(state, tail, width)
+        span *= RADIX
+    return state
 
 
 def on_device(grad_out, w_out, queries, keys_in, values, log_decay, kv_state):
@@ -49,9 +59,16 @@
         "thd,the->hde", scaled_q, grad_attn, preferred_element_type=jnp.float32
     )
     block_decay = jnp.exp(block_total)
-    identity = (jnp.ones((head_count,), jnp.float32), jnp.zeros_like(block_terms))
-    combined = entering((block_decay, block_terms), "seq", merge_states, identity)
-    future_low = combined[1].astype(jnp.bfloat16)
+    width = head_size * head_size
+    packed = jnp.concatenate(
+        [
+            block_terms.reshape(head_count, width),
+            jnp.broadcast_to(block_decay[:, None], (head_count, 128)),
+        ],
+        axis=1,
+    )
+    combined = entering_after(packed, "seq", width)
+    future_low = combined[:, :width].reshape(head_count, head_size, head_size).astype(jnp.bfloat16)
     log_gaps = cumul[:, :, None] - cumul[:, None, :]
     rows_idx = lax.broadcasted_iota(jnp.int32, (length_dev, length_dev), 0)
     cols_idx = lax.broadcasted_iota(jnp.int32, (length_dev, length_dev), 1)

time: 1150 us -> 153 us (0.13)
  the two profiles are of different devices: /device:TPU:1 before, /device:TPU:18 now
where the time goes in v1:
time: 153 us
  waiting for transfers between devices  85.1 us (56%)
  starting transfers between devices  41.7 us (27%)
  between operations  14.3 us (9%)
  local copies, waits for them, and re-layouts  6.64 us (4%)
  matrix products  3.42 us (2%)
  other arithmetic  1.57 us (1%)
    all_gather x1, waiting for transfers between devices, on_device(): lax.all_gather(w_out, 'dp', axis=1, tiled=True)  58 us
    ppermute x13, starting transfers between devices, shifted(): return lax.ppermute(array, axis, pairs)  41.6 us
    ppermute x13, waiting for transfers between devices, shifted(): return lax.ppermute(array, axis, pairs)  26.5 us
    unnamed x10, local copies, waits for them, and re-layouts  4.81 us
  transfers between devices with their start and end apart: 14, of which 7 were waited for; matrix products, arithmetic and copies ran while one was open for 4% of the time, Pallas kernels for 0%

profile of v1, /device:TPU:18, one launch (start us, length us, event | category | flops | bytes accessed | tf_op | source)
XLA Modules:
  0.0 152.7 jit_solution(5806421049468689563)
XLA Ops:
  7.2 0.7 all-gather.2.cloned.1.call-update
  7.9 0.9 copy.39
  8.8 0.9 copy.38
  9.7 0.9 copy.37
  10.5 1.0 reduce_window_sum.11
  11.5 0.2 slice_reduce_fusion.12
  11.8 58.0 %all-gather.2.cloned.1.call-done = bf16[128,6144]{1,0:T(8,128)(2,1)} async-done(((bf16[128,1536]{1,0:T(8,128)(2,1)}), bf16[128,6144]{1,0:T(8,128)(2,1)}) %all-gather.2.cloned.1.call-update) | async-done | bytes 1572880 | tf_op jit(solution)/shard_map/all_gather | solution.py:46
  69.8 2.0 %fusion.15 = bf16[128,128]{0,1:T(8,128)(2,1)S(1)} fusion(bf16[128,6144]{1,0:T(8,128)(2,1)} %all-gather.2.cloned.1.call-done, bf16[1,128,6144]{2,1,0:T(8,128)(2,1)S(1)} %copy-done), kind=kOutput, calls=%fused_computation.22 | convolution fusion | flops 201342976 | bytes 3178496 | tf_op jit(solution)/shard_map/dot_general | solution.py:44
  71.8 0.1 fusion.22
  72.1 8.7 %collective-permute-start.3 = (f32[2,4224]{1,0:T(2,128)S(1)}, f32[2,4224]{1,0:T(2,128)S(1)}, u32[]{:S(2)}, u32[]{:S(2)}) collective-permute-start(f32[2,4224]{1,0:T(2,128)S(1)} %pad_maximum_fusion), channel_id=1, source_target_pairs={{4,0},{5,1},{6,2},{7,3},{8,4},{9,5},{10,6},{11,7},{12,8},{13,9},{1... | collective-permute-start | bytes 101384 | tf_op jit(solution)/shard_map/ppermute | solution.py:11
  80.8 3.3 %collective-permute-start.2 = (f32[2,4224]{1,0:T(2,128)S(1)}, f32[2,4224]{1,0:T(2,128)S(1)}, u32[]{:S(2)}, u32[]{:S(2)}) collective-permute-start(f32[2,4224]{1,0:T(2,128)S(1)} %pad_maximum_fusion), channel_id=1, source_target_pairs={{3,0},{4,1},{5,2},{6,3},{7,4},{8,5},{9,6},{10,7},{11,8},{12,9},{13... | collective-permute-start | bytes 101384 | tf_op jit(solution)/shard_map/ppermute | solution.py:11
  84.2 3.3 %collective-permute-start.1 = (f32[2,4224]{1,0:T(2,128)S(1)}, f32[2,4224]{1,0:T(2,128)S(1)}, u32[]{:S(2)}, u32[]{:S(2)}) collective-permute-start(f32[2,4224]{1,0:T(2,128)S(1)} %pad_maximum_fusion), channel_id=1, source_target_pairs={{2,0},{3,1},{4,2},{5,3},{6,4},{7,5},{8,6},{9,7},{10,8},{11,9},{12,... | collective-permute-start | bytes 101384 | tf_op jit(solution)/shard_map/ppermute | solution.py:11
  87.5 2.8 %collective-permute-start = (f32[2,4224]{1,0:T(2,128)S(1)}, f32[2,4224]{1,0:T(2,128)S(1)}, u32[]{:S(2)}, u32[]{:S(2)}) collective-permute-start(f32[2,4224]{1,0:T(2,128)S(1)} %pad_maximum_fusion), channel_id=1, source_target_pairs={{1,0},{2,1},{3,2},{4,3},{5,4},{6,5},{7,6},{8,7},{9,8},{10,9},{11,1... | collective-permute-start | bytes 101384 | tf_op jit(solution)/shard_map/ppermute | solution.py:11
  90.3 0.2 fusion.2
  90.5 0.1 convolution_bitcast_fusion.4
  90.6 0.1 fusion.12
  90.8 0.7 copy.41
  91.5 0.1 slice_reduce_fusion.6
  91.6 0.1 slice_reduce_fusion.7
  91.8 0.1 slice_reduce_fusion.8
  92.1 2.3 %collective-permute-start.5 = (f32[2,4224]{1,0:T(2,128)S(1)}, f32[2,4224]{1,0:T(2,128)S(1)}, u32[]{:S(2)}, u32[]{:S(2)}) collective-permute-start(f32[2,4224]{1,0:T(2,128)S(1)} %pad_maximum_fusion.1), channel_id=1, source_target_pairs={{8,0},{9,1},{10,2},{11,3},{12,4},{13,5},{14,6},{15,7},{16,8},{17,9... | collective-permute-start | bytes 101384 | tf_op jit(solution)/shard_map/ppermute | solution.py:11
  94.4 0.1 slice_reduce_fusion.11
  94.5 10.3 %collective-permute-start.6 = (f32[2,4224]{1,0:T(2,128)S(1)}, f32[2,4224]{1,0:T(2,128)S(1)}, u32[]{:S(2)}, u32[]{:S(2)}) collective-permute-start(f32[2,4224]{1,0:T(2,128)S(1)} %pad_maximum_fusion.1), channel_id=1, source_target_pairs={{12,0},{13,1},{14,2},{15,3},{16,4},{17,5},{18,6},{19,7},{20,8},{21... | collective-permute-start | bytes 101384 | tf_op jit(solution)/shard_map/ppermute | solution.py:11
  104.8 1.9 %collective-permute-start.4 = (f32[2,4224]{1,0:T(2,128)S(1)}, f32[2,4224]{1,0:T(2,128)S(1)}, u32[]{:S(2)}, u32[]{:S(2)}) collective-permute-start(f32[2,4224]{1,0:T(2,128)S(1)} %pad_maximum_fusion.1), channel_id=1, source_target_pairs={{4,0},{5,1},{6,2},{7,3},{8,4},{9,5},{10,6},{11,7},{12,8},{13,9},{1... | collective-permute-start | bytes 101384 | tf_op jit(solution)/shard_map/ppermute | solution.py:11
  106.8 0.1 slice_reduce_fusion.4
  106.9 4.7 %collective-permute-done.4 = f32[2,4224]{1,0:T(2,128)S(1)} collective-permute-done((f32[2,4224]{1,0:T(2,128)S(1)}, f32[2,4224]{1,0:T(2,128)S(1)}, u32[]{:S(2)}, u32[]{:S(2)}) %collective-permute-start.4) | collective-permute-done | bytes 33824 | tf_op jit(solution)/shard_map/ppermute | solution.py:11
  111.5 0.1 slice_reduce_fusion.5
  111.8 1.9 %collective-permute-start.8 = (f32[2,4224]{1,0:T(2,128)S(1)}, f32[2,4224]{1,0:T(2,128)S(1)}, u32[]{:S(2)}, u32[]{:S(2)}) collective-permute-start(f32[2,4224]{1,0:T(2,128)S(1)} %pad_maximum_fusion.2), channel_id=1, source_target_pairs={{32,0},{33,1},{34,2},{35,3},{36,4},{37,5},{38,6},{39,7},{40,8},{41... | collective-permute-start | bytes 101384 | tf_op jit(solution)/shard_map/ppermute | solution.py:11
  113.7 0.1 slice_reduce_fusion.10
  113.8 1.3 collective-permute-start.9
  115.1 1.9 %collective-permute-start.7 = (f32[2,4224]{1,0:T(2,128)S(1)}, f32[2,4224]{1,0:T(2,128)S(1)}, u32[]{:S(2)}, u32[]{:S(2)}) collective-permute-start(f32[2,4224]{1,0:T(2,128)S(1)} %pad_maximum_fusion.2), channel_id=1, source_target_pairs={{16,0},{17,1},{18,2},{19,3},{20,4},{21,5},{22,6},{23,7},{24,8},{25... | collective-permute-start | bytes 101384 | tf_op jit(solution)/shard_map/ppermute | solution.py:11
  117.1 0.9 collective-permute-done.8
  117.9 0.1 slice_reduce_fusion.2
  118.1 7.6 %collective-permute-done.7 = f32[2,4224]{1,0:T(2,128)S(1)} collective-permute-done((f32[2,4224]{1,0:T(2,128)S(1)}, f32[2,4224]{1,0:T(2,128)S(1)}, u32[]{:S(2)}, u32[]{:S(2)}) %collective-permute-start.7) | collective-permute-done | bytes 33824 | tf_op jit(solution)/shard_map/ppermute | solution.py:11
  125.7 0.1 slice_reduce_fusion.3
  125.9 1.3 collective-permute-start.11
  127.2 0.1 slice_reduce_fusion.9
  127.3 1.3 collective-permute-start.12
  128.6 1.3 collective-permute-start.10
  129.9 11.4 %collective-permute-done.11 = f32[2,4224]{1,0:T(2,128)S(1)} collective-permute-done((f32[2,4224]{1,0:T(2,128)S(1)}, f32[2,4224]{1,0:T(2,128)S(1)}, u32[]{:S(2)}, u32[]{:S(2)}) %collective-permute-start.11) | collective-permute-done | bytes 33824 | tf_op jit(solution)/shard_map/ppermute | solution.py:11
  141.4 0.1 slice_reduce_fusion.1
  141.5 1.9 %collective-permute-done.12 = f32[2,4224]{1,0:T(2,128)S(1)} collective-permute-done((f32[2,4224]{1,0:T(2,128)S(1)}, f32[2,4224]{1,0:T(2,128)S(1)}, u32[]{:S(2)}, u32[]{:S(2)}) %collective-permute-start.12) | collective-permute-done | bytes 33824 | tf_op jit(solution)/shard_map/ppermute | solution.py:11
  143.6 0.1 fusion.11
  143.7 0.2 fusion.10
  143.9 0.1 fusion.13
  144.1 0.7 copy.42
  144.8 0.3 fusion.14
  145.1 0.7 copy.43
  (30 shorter events, 1.1 us)
Async XLA Ops:
  7.2 62.6 %copy-start = (bf16[1,128,6144]{2,1,0:T(8,128)(2,1)S(1)}, bf16[1,128,6144]{2,1,0:T(8,128)(2,1)}, u32[]{:S(2)}) copy-start(bf16[1,128,6144]{2,1,0:T(8,128)(2,1)} %param.7) | copy-start | bytes 4718596
  7.2 62.6 %all-gather.2.cloned.1.call-start = ((), (), s32[]{:S(2)}) async-start(), calls=%async_computation | async-start | bytes 1966080 | tf_op jit(solution)/shard_map/all_gather | solution.py:46
  11.8 78.8 %copy-start.1 = (bf16[1,1,2,64,64]{4,3,2,1,0:T(8,128)(2,1)S(1)}, bf16[1,1,2,64,64]{4,3,2,1,0:T(8,128)(2,1)}, u32[]{:S(2)}) copy-start(bf16[1,1,2,64,64]{4,3,2,1,0:T(8,128)(2,1)} %param.13) | copy-start | bytes 49156
  72.1 19.9 %collective-permute-start.3 = (f32[2,4224]{1,0:T(2,128)S(1)}, f32[2,4224]{1,0:T(2,128)S(1)}, u32[]{:S(2)}, u32[]{:S(2)}) collective-permute-start(f32[2,4224]{1,0:T(2,128)S(1)} %pad_maximum_fusion), channel_id=1, source_target_pairs={{4,0},{5,1},{6,2},{7,3},{8,4},{9,5},{10,6},{11,7},{12,8},{13,9},{1... | collective-permute-start | bytes 101384 | tf_op jit(solution)/shard_map/ppermute | solution.py:11
  80.8 10.7 %collective-permute-start.2 = (f32[2,4224]{1,0:T(2,128)S(1)}, f32[2,4224]{1,0:T(2,128)S(1)}, u32[]{:S(2)}, u32[]{:S(2)}) collective-permute-start(f32[2,4224]{1,0:T(2,128)S(1)} %pad_maximum_fusion), channel_id=1, source_target_pairs={{3,0},{4,1},{5,2},{6,3},{7,4},{8,5},{9,6},{10,7},{11,8},{12,9},{13... | collective-permute-start | bytes 101384 | tf_op jit(solution)/shard_map/ppermute | solution.py:11
  84.2 7.5 %collective-permute-start.1 = (f32[2,4224]{1,0:T(2,128)S(1)}, f32[2,4224]{1,0:T(2,128)S(1)}, u32[]{:S(2)}, u32[]{:S(2)}) collective-permute-start(f32[2,4224]{1,0:T(2,128)S(1)} %pad_maximum_fusion), channel_id=1, source_target_pairs={{2,0},{3,1},{4,2},{5,3},{6,4},{7,5},{8,6},{9,7},{10,8},{11,9},{12,... | collective-permute-start | bytes 101384 | tf_op jit(solution)/shard_map/ppermute | solution.py:11
  87.5 4.3 %collective-permute-start = (f32[2,4224]{1,0:T(2,128)S(1)}, f32[2,4224]{1,0:T(2,128)S(1)}, u32[]{:S(2)}, u32[]{:S(2)}) collective-permute-start(f32[2,4224]{1,0:T(2,128)S(1)} %pad_maximum_fusion), channel_id=1, source_target_pairs={{1,0},{2,1},{3,2},{4,3},{5,4},{6,5},{7,6},{8,7},{9,8},{10,9},{11,1... | collective-permute-start | bytes 101384 | tf_op jit(solution)/shard_map/ppermute | solution.py:11
  92.1 14.6 %collective-permute-start.5 = (f32[2,4224]{1,0:T(2,128)S(1)}, f32[2,4224]{1,0:T(2,128)S(1)}, u32[]{:S(2)}, u32[]{:S(2)}) collective-permute-start(f32[2,4224]{1,0:T(2,128)S(1)} %pad_maximum_fusion.1), channel_id=1, source_target_pairs={{8,0},{9,1},{10,2},{11,3},{12,4},{13,5},{14,6},{15,7},{16,8},{17,9... | collective-permute-start | bytes 101384 | tf_op jit(solution)/shard_map/ppermute | solution.py:11
  94.5 17.1 %collective-permute-start.6 = (f32[2,4224]{1,0:T(2,128)S(1)}, f32[2,4224]{1,0:T(2,128)S(1)}, u32[]{:S(2)}, u32[]{:S(2)}) collective-permute-start(f32[2,4224]{1,0:T(2,128)S(1)} %pad_maximum_fusion.1), channel_id=1, source_target_pairs={{12,0},{13,1},{14,2},{15,3},{16,4},{17,5},{18,6},{19,7},{20,8},{21... | collective-permute-start | bytes 101384 | tf_op jit(solution)/shard_map/ppermute | solution.py:11
  104.8 6.7 %collective-permute-start.4 = (f32[2,4224]{1,0:T(2,128)S(1)}, f32[2,4224]{1,0:T(2,128)S(1)}, u32[]{:S(2)}, u32[]{:S(2)}) collective-permute-start(f32[2,4224]{1,0:T(2,128)S(1)} %pad_maximum_fusion.1), channel_id=1, source_target_pairs={{4,0},{5,1},{6,2},{7,3},{8,4},{9,5},{10,6},{11,7},{12,8},{13,9},{1... | collective-permute-start | bytes 101384 | tf_op jit(solution)/shard_map/ppermute | solution.py:11
  111.8 6.1 %collective-permute-start.8 = (f32[2,4224]{1,0:T(2,128)S(1)}, f32[2,4224]{1,0:T(2,128)S(1)}, u32[]{:S(2)}, u32[]{:S(2)}) collective-permute-start(f32[2,4224]{1,0:T(2,128)S(1)} %pad_maximum_fusion.2), channel_id=1, source_target_pairs={{32,0},{33,1},{34,2},{35,3},{36,4},{37,5},{38,6},{39,7},{40,8},{41... | collective-permute-start | bytes 101384 | tf_op jit(solution)/shard_map/ppermute | solution.py:11
  113.8 11.9 %collective-permute-start.9 = (f32[2,4224]{1,0:T(2,128)S(1)}, f32[2,4224]{1,0:T(2,128)S(1)}, u32[]{:S(2)}, u32[]{:S(2)}) collective-permute-start(f32[2,4224]{1,0:T(2,128)S(1)} %pad_maximum_fusion.2), channel_id=1, source_target_pairs={{48,0},{49,1},{50,2},{51,3},{52,4},{53,5},{54,6},{55,7},{56,8},{57... | collective-permute-start | bytes 101384 | tf_op jit(solution)/shard_map/ppermute | solution.py:11
  115.1 10.5 %collective-permute-start.7 = (f32[2,4224]{1,0:T(2,128)S(1)}, f32[2,4224]{1,0:T(2,128)S(1)}, u32[]{:S(2)}, u32[]{:S(2)}) collective-permute-start(f32[2,4224]{1,0:T(2,128)S(1)} %pad_maximum_fusion.2), channel_id=1, source_target_pairs={{16,0},{17,1},{18,2},{19,3},{20,4},{21,5},{22,6},{23,7},{24,8},{25... | collective-permute-start | bytes 101384 | tf_op jit(solution)/shard_map/ppermute | solution.py:11
  125.9 15.4 %collective-permute-start.11 = (f32[2,4224]{1,0:T(2,128)S(1)}, f32[2,4224]{1,0:T(2,128)S(1)}, u32[]{:S(2)}, u32[]{:S(2)}) collective-permute-start(f32[2,4224]{1,0:T(2,128)S(1)} %pad_maximum_fusion.3), channel_id=1, source_target_pairs={{128,0},{129,1},{130,2},{131,3},{132,4},{133,5},{134,6},{135,7},{1... | collective-permute-start | bytes 101384 | tf_op jit(solution)/shard_map/ppermute | solution.py:11
  127.3 16.1 %collective-permute-start.12 = (f32[2,4224]{1,0:T(2,128)S(1)}, f32[2,4224]{1,0:T(2,128)S(1)}, u32[]{:S(2)}, u32[]{:S(2)}) collective-permute-start(f32[2,4224]{1,0:T(2,128)S(1)} %pad_maximum_fusion.3), channel_id=1, source_target_pairs={{192,0},{193,1},{194,2},{195,3},{196,4},{197,5},{198,6},{199,7},{2... | collective-permute-start | bytes 101384 | tf_op jit(solution)/shard_map/ppermute | solution.py:11
  128.6 12.8 %collective-permute-start.10 = (f32[2,4224]{1,0:T(2,128)S(1)}, f32[2,4224]{1,0:T(2,128)S(1)}, u32[]{:S(2)}, u32[]{:S(2)}) collective-permute-start(f32[2,4224]{1,0:T(2,128)S(1)} %pad_maximum_fusion.3), channel_id=1, source_target_pairs={{64,0},{65,1},{66,2},{67,3},{68,4},{69,5},{70,6},{71,7},{72,8},{73... | collective-permute-start | bytes 101384 | tf_op jit(solution)/shard_map/ppermute | solution.py:11
Sparse Core Ops, SparseCore 0:
  10.7 59.0 all-gather.1

commit v2 on v1

--- a/solution.py
+++ b/solution.py
@@ -36,17 +36,101 @@
     return state
 
 
+def entering_by_transpose(block_terms, block_total, axis):
+    size = lax.axis_size(axis)
+    heads, rows, cols = block_terms.shape
+    piece = heads * rows * cols // size
+    owner_head = (jnp.arange(size) * piece) // (rows * cols)
+    payload = jnp.concatenate(
+        [block_terms.reshape(size, piece), block_total[owner_head][:, None]], axis=1
+    )
+    gathered = lax.all_to_all(payload, axis, 0, 0, tiled=True)
+    totals = gathered[:, piece]
+    later = lax.broadcasted_iota(jnp.int32, (size, size), 1) > lax.broadcasted_iota(
+        jnp.int32, (size, size), 0
+    )
+    between = jnp.dot(
+        jnp.where(later, totals[None, :], 0.0),
+        later.astype(jnp.float32),
+        precision=lax.Precision.HIGHEST,
+    )
+    weights = jnp.where(later, jnp.exp(jnp.where(later, between, 0.0)), 0.0)
+    folded = jnp.dot(weights, gathered[:, :piece], precision=lax.Precision.HIGHEST)
+    returned = lax.all_to_all(folded, axis, 0, 0, tiled=True)
+    return returned.reshape(heads, rows, cols)
+
+
+Z_HI = 2
+X_SIZE = 8
+Y_SIZE = 8
+CORES = 2
+
+
+def linear(z, x, y, core, z_lo_size):
+    seq = ((x * Z_HI + z // z_lo_size) * Y_SIZE + y) * CORES + core
+    return (z % z_lo_size) * (X_SIZE * Z_HI * Y_SIZE * CORES) + seq
+
+
+def from_offset(array, distance, z_lo_size):
+    z_size = z_lo_size * Z_HI
+    pairs = []
+    for z in range(z_size):
+        for x in range(X_SIZE):
+            for y in range(Y_SIZE):
+                for core in range(CORES):
+                    src = linear((z + distance) % z_size, x, y, core, z_lo_size)
+                    pairs.append((src, linear(z, x, y, core, z_lo_size)))
+    return lax.ppermute(array, ("dp", "seq"), pairs)
+
+
+def partial_product(token_rows, block, index, cols):
+    rows = lax.dynamic_slice_in_dim(token_rows, index * cols, cols, axis=1)
+    return lax.dot_general(rows, block, (((1,), (1,)), ((), ())), preferred_element_type=jnp.float32)
+
+
+def project(token_rows, w_local):
+    z_lo_size = lax.axis_size("dp")
+    z_lo = lax.axis_index("dp")
+    core = lax.axis_index("seq") % CORES
+    cols = w_local.shape[1]
+    half = w_local.shape[0] // CORES
+    quarter = half // 2
+    mine = lax.dynamic_slice_in_dim(w_local, core * half, half, 0)
+    theirs = lax.dynamic_slice_in_dim(w_local, (1 - core) * half, half, 0)
+    near_up = from_offset(mine, 1, z_lo_size)
+    near_down = from_offset(mine, -1, z_lo_size)
+    far = jnp.concatenate(
+        [
+            from_offset(mine[:quarter], 2, z_lo_size),
+            from_offset(mine[quarter:], -2, z_lo_size),
+        ],
+        axis=0,
+    )
+    fetched = [near_up, near_down, far]
+    offsets = [1, z_lo_size - 1, 2]
+    swapped = lax.ppermute(
+        jnp.stack(fetched), "seq",
+        [(i, i ^ 1) for i in range(lax.axis_size("seq"))],
+    )
+    own_mine = partial_product(token_rows, mine, z_lo, cols)
+    own_theirs = partial_product(token_rows, theirs, z_lo, cols)
+    for k in range(3):
+        index = (z_lo + offsets[k]) % z_lo_size
+        own_mine = own_mine + partial_product(token_rows, fetched[k], index, cols)
+        own_theirs = own_theirs + partial_product(token_rows, swapped[k], index, cols)
+    return jnp.where(
+        core == 0,
+        jnp.concatenate([own_mine, own_theirs], axis=1),
+        jnp.concatenate([own_theirs, own_mine], axis=1),
+    )
+
+
 def on_device(grad_out, w_out, queries, keys_in, values, log_decay, kv_state):
     token_rows = grad_out[0]
     length_dev = token_rows.shape[0]
     head_count = log_decay.shape[1]
     head_size = queries.shape[2] // head_count
-    projected = lax.dot_general(
-        token_rows,
-        lax.all_gather(w_out, "dp", axis=1, tiled=True),
-        (((1,), (1,)), ((), ())),
-        preferred_element_type=jnp.float32,
-    )
+    projected = project(token_rows, w_out)
     grad_attn = projected.astype(jnp.bfloat16).reshape(length_dev, head_count, head_size)
     query_heads = queries[0].reshape(length_dev, head_count, head_size)
     key_heads = keys_in[0].reshape(length_dev, head_count, head_size)
@@ -67,8 +151,8 @@
         ],
         axis=1,
     )
-    combined = entering_after(packed, "seq", width)
-    future_low = combined[:, :width].reshape(head_count, head_size, head_size).astype(jnp.bfloat16)
+    future = entering_by_transpose(block_terms, block_total, "seq")
+    future_low = future.astype(jnp.bfloat16)
     log_gaps = cumul[:, :, None] - cumul[:, None, :]
     rows_idx = lax.broadcasted_iota(jnp.int32, (length_dev, length_dev), 0)
     cols_idx = lax.broadcasted_iota(jnp.int32, (length_dev, length_dev), 1)

time: 153 us -> 105 us (0.69)
  the two profiles are of different devices: /device:TPU:18 before, /device:TPU:1 now
where the time goes in v2:
time: 105 us; the launch traced here: 104 us
  starting transfers between devices  55 us (52%)
  waiting for transfers between devices  34.1 us (32%)
  local copies, waits for them, and re-layouts  6.14 us (6%)
  matrix products  4.18 us (4%)
  other arithmetic  4.03 us (4%)
    ppermute x4, starting transfers between devices, from_offset(): return lax.ppermute(array, ('dp', 'seq'), pairs)  26 us
    all_to_all x1, waiting for transfers between devices, entering_by_transpose(): gathered = lax.all_to_all(payload, axis, 0, 0, tiled=True)  16.6 us
    all_to_all x1, waiting for transfers between devices, entering_by_transpose(): returned = lax.all_to_all(folded, axis, 0, 0, tiled=True)  16.2 us
    all_to_all x1, starting transfers between devices, entering_by_transpose(): gathered = lax.all_to_all(payload, axis, 0, 0, tiled=True)  15.7 us
    all_to_all x1, starting transfers between devices, entering_by_transpose(): returned = lax.all_to_all(folded, axis, 0, 0, tiled=True)  7.8 us
    ppermute x1, starting transfers between devices, project(): lax.ppermute(jnp.stack(fetched), 'seq', [(i, i ^ 1) for i in range(lax.ax...  5.48 us
    unnamed x19, local copies, waits for them, and re-layouts  2.58 us
  transfers between devices with their start and end apart: 7, of which 4 were waited for; matrix products, arithmetic and copies ran while one was open for 7% of the time, Pallas kernels for 0%

profile of v2, /device:TPU:1, one launch (start us, length us, event | category | flops | bytes accessed | tf_op | source)
XLA Modules:
  0.0 104.5 jit_solution(17006767663558776239)
XLA Ops:
  0.7 1.1 %constant_dynamic-slice_fusion.2 = bf16[64,1536]{1,0:T(8,128)(2,1)S(1)} fusion(bf16[128,1536]{1,0:T(8,128)(2,1)} %param.8, s32[]{:T(128)S(6)} %select_n.93), kind=kLoop, calls=%fused_computation.100 | loop fusion | bytes 393220 | tf_op jit(solution)/shard_map/dynamic_slice | solution.py:98
  1.8 17.9 %collective-permute-start = (bf16[64,1536]{1,0:T(8,128)(2,1)S(1)}, bf16[64,1536]{1,0:T(8,128)(2,1)S(1)}, u32[]{:S(2)}, u32[]{:S(2)}) collective-permute-start(bf16[64,1536]{1,0:T(8,128)(2,1)S(1)} %constant_dynamic-slice_fusion.2), channel_id=1, source_target_pairs={{256,0},{257,1},{258,2},{259,3},{260,4},{261,5},{262,6},{263,7},{2... | collective-permute-start | bytes 589832 | tf_op jit(solution)/shard_map/ppermute | solution.py:83
  19.7 1.9 %collective-permute-start.1 = (bf16[64,1536]{1,0:T(8,128)(2,1)S(1)}, bf16[64,1536]{1,0:T(8,128)(2,1)S(1)}, u32[]{:S(2)}, u32[]{:S(2)}) collective-permute-start(bf16[64,1536]{1,0:T(8,128)(2,1)S(1)} %constant_dynamic-slice_fusion.2), channel_id=1, source_target_pairs={{784,0},{785,1},{786,2},{787,3},{788,4},{789,5},{790,6},{791,7},{7... | collective-permute-start | bytes 589832 | tf_op jit(solution)/shard_map/ppermute | solution.py:83
  21.6 1.0 constant_dynamic-slice_fusion
  22.5 3.1 %collective-permute-start.2 = (bf16[32,1536]{1,0:T(8,128)(2,1)S(1)}, bf16[32,1536]{1,0:T(8,128)(2,1)S(1)}, u32[]{:S(2)}, u32[]{:S(2)}) collective-permute-start(bf16[32,1536]{1,0:T(8,128)(2,1)S(1)} %get-tuple-element.16), channel_id=1, source_target_pairs={{512,0},{513,1},{514,2},{515,3},{516,4},{517,5},{518,6},{519,7},{5... | collective-permute-start | bytes 294920 | tf_op jit(solution)/shard_map/ppermute | solution.py:83
  25.6 3.1 %collective-permute-start.3 = (bf16[32,1536]{1,0:T(8,128)(2,1)S(1)}, bf16[32,1536]{1,0:T(8,128)(2,1)S(1)}, u32[]{:S(2)}, u32[]{:S(2)}) collective-permute-start(bf16[32,1536]{1,0:T(8,128)(2,1)S(1)} %get-tuple-element.15), channel_id=1, source_target_pairs={{528,0},{529,1},{530,2},{531,3},{532,4},{533,5},{534,6},{535,7},{5... | collective-permute-start | bytes 294920 | tf_op jit(solution)/shard_map/ppermute | solution.py:83
  28.8 1.0 reduce_window_sum.11
  29.8 0.2 slice_reduce_fusion.1
  30.0 0.6 fusion.68
  30.6 0.2 fusion.29
  30.8 0.3 fusion.27
  31.1 0.1 exponential_bitcast_fusion
  31.2 0.1 copy.39
  31.3 0.1 copy.38
  31.4 0.1 copy.37
  31.6 1.4 %fusion.48 = f32[256,1]{1,0:T(8,128)S(1)} fusion(f32[]{:T(128)} %bitcast.24, f32[]{:T(128)} %bitcast.23), kind=kLoop, calls=%fused_computation.76 | loop fusion | flops 5376 | bytes 1032 | tf_op jit(solution)/shard_map/gather | solution.py:45
  33.0 0.6 collective-permute-done.3
  33.7 5.5 %collective-permute-start.4 = (bf16[3,64,1536]{2,1,0:T(8,128)(2,1)S(1)}, bf16[3,64,1536]{2,1,0:T(8,128)(2,1)S(1)}, u32[]{:S(2)}, u32[]{:S(2)}) collective-permute-start(bf16[3,64,1536]{2,1,0:T(8,128)(2,1)S(1)} %pad_maximum_fusion), channel_id=1, source_target_pairs={{0,1},{1,0},{2,3},{3,2},{4,5},{5,4},{6,7},{7,6},{8,9},{9,8},{10,11... | collective-permute-start | bytes 1769480 | tf_op jit(solution)/shard_map/ppermute | solution.py:111
  39.2 0.3 fusion.21
  39.5 0.3 convolution_add_fusion.3
  39.8 0.3 fusion.16
  40.0 0.8 collective-permute-done.4
  40.8 0.2 fusion.19
  41.1 0.3 convolution_add_fusion.1
  41.4 0.3 fusion.18
  41.6 0.1 fusion.55
  41.8 0.1 reshape.133
  41.9 0.8 pad_maximum_fusion.1
  42.6 15.7 %all-to-all-start = ((f32[256,1,33]{2,1,0:T(1,128)}), f32[256,1,33]{2,1,0:T(1,128)S(1)}, u32[]{:S(2)}, u32[]{:S(2)}) async-start(f32[256,1,33]{2,1,0:T(1,128)} %bitcast.26), calls=%async_computation | async-start | bytes 262144 | tf_op jit(solution)/shard_map/all_to_all | solution.py:47
  58.3 0.2 fusion.2
  58.6 0.1 convolution_bitcast_fusion.4
  58.7 16.6 %all-to-all-done = f32[256,1,33]{2,1,0:T(1,128)S(1)} async-done(((f32[256,1,33]{2,1,0:T(1,128)}), f32[256,1,33]{2,1,0:T(1,128)S(1)}, u32[]{:S(2)}, u32[]{:S(2)}) %all-to-all-start) | async-done | bytes 33824 | tf_op jit(solution)/shard_map/all_to_all | solution.py:47
  75.3 0.2 slice_reduce_fusion
  75.5 0.3 fusion.1
  75.8 0.4 fusion.43
  76.1 0.7 convert
  76.9 7.8 %all-to-all-start.1 = ((bf16[256,1,32]{2,1,0:T(2,128)(2,1)}), bf16[256,1,32]{2,1,0:T(2,128)(2,1)S(1)}, u32[]{:S(2)}, u32[]{:S(2)}) async-start(bf16[256,1,32]{2,1,0:T(2,128)(2,1)} %convert), calls=%async_computation.1 | async-start | bytes 262144 | tf_op jit(solution)/shard_map/all_to_all | solution.py:59
  84.7 0.1 fusion.12
  84.8 0.7 copy.43
  85.6 16.2 %all-to-all-done.1 = bf16[256,1,32]{2,1,0:T(2,128)(2,1)S(1)} async-done(((bf16[256,1,32]{2,1,0:T(2,128)(2,1)}), bf16[256,1,32]{2,1,0:T(2,128)(2,1)S(1)}, u32[]{:S(2)}, u32[]{:S(2)}) %all-to-all-start.1) | async-done | bytes 16416 | tf_op jit(solution)/shard_map/all_to_all | solution.py:59
  101.7 0.4 convert_reduce_fusion
  102.1 0.1 convert_element_type.72
  102.2 0.2 fusion.10
  102.4 0.1 fusion.11
  102.5 0.3 fusion.14
  102.9 0.7 copy.45
  103.6 0.1 fusion.13
  103.8 0.7 copy.44
  (19 shorter events, 0.1 us)
Async XLA Ops:
  0.6 29.9 %copy-start = (bf16[1,128,6144]{2,1,0:T(8,128)(2,1)S(1)}, bf16[1,128,6144]{2,1,0:T(8,128)(2,1)}, u32[]{:S(2)}) copy-start(bf16[1,128,6144]{2,1,0:T(8,128)(2,1)} %param.7) | copy-start | bytes 4718596
  0.6 30.2 %copy-start.1 = (bf16[128,1536]{1,0:T(8,128)(2,1)S(1)}, bf16[128,1536]{1,0:T(8,128)(2,1)}, u32[]{:S(2)}) copy-start(bf16[128,1536]{1,0:T(8,128)(2,1)} %param.8) | copy-start | bytes 1179652
  0.7 30.5 %copy-start.2 = (bf16[1,128,128]{2,1,0:T(8,128)(2,1)S(1)}, bf16[1,128,128]{2,1,0:T(8,128)(2,1)}, u32[]{:S(2)}) copy-start(bf16[1,128,128]{2,1,0:T(8,128)(2,1)} %param.9) | copy-start | bytes 98308
  0.7 30.6 %copy-start.3 = (bf16[1,128,128]{2,1,0:T(8,128)(2,1)S(1)}, bf16[1,128,128]{2,1,0:T(8,128)(2,1)}, u32[]{:S(2)}) copy-start(bf16[1,128,128]{2,1,0:T(8,128)(2,1)} %param.10) | copy-start | bytes 98308
  0.7 30.7 %copy-start.4 = (bf16[1,128,128]{2,1,0:T(8,128)(2,1)S(1)}, bf16[1,128,128]{2,1,0:T(8,128)(2,1)}, u32[]{:S(2)}) copy-start(bf16[1,128,128]{2,1,0:T(8,128)(2,1)} %param.11) | copy-start | bytes 98308
  1.8 31.9 %collective-permute-start = (bf16[64,1536]{1,0:T(8,128)(2,1)S(1)}, bf16[64,1536]{1,0:T(8,128)(2,1)S(1)}, u32[]{:S(2)}, u32[]{:S(2)}) collective-permute-start(bf16[64,1536]{1,0:T(8,128)(2,1)S(1)} %constant_dynamic-slice_fusion.2), channel_id=1, source_target_pairs={{256,0},{257,1},{258,2},{259,3},{260,4},{261,5},{262,6},{263,7},{2... | collective-permute-start | bytes 589832 | tf_op jit(solution)/shard_map/ppermute | solution.py:83
  19.7 14.0 %collective-permute-start.1 = (bf16[64,1536]{1,0:T(8,128)(2,1)S(1)}, bf16[64,1536]{1,0:T(8,128)(2,1)S(1)}, u32[]{:S(2)}, u32[]{:S(2)}) collective-permute-start(bf16[64,1536]{1,0:T(8,128)(2,1)S(1)} %constant_dynamic-slice_fusion.2), channel_id=1, source_target_pairs={{784,0},{785,1},{786,2},{787,3},{788,4},{789,5},{790,6},{791,7},{7... | collective-permute-start | bytes 589832 | tf_op jit(solution)/shard_map/ppermute | solution.py:83
  22.5 10.5 %collective-permute-start.2 = (bf16[32,1536]{1,0:T(8,128)(2,1)S(1)}, bf16[32,1536]{1,0:T(8,128)(2,1)S(1)}, u32[]{:S(2)}, u32[]{:S(2)}) collective-permute-start(bf16[32,1536]{1,0:T(8,128)(2,1)S(1)} %get-tuple-element.16), channel_id=1, source_target_pairs={{512,0},{513,1},{514,2},{515,3},{516,4},{517,5},{518,6},{519,7},{5... | collective-permute-start | bytes 294920 | tf_op jit(solution)/shard_map/ppermute | solution.py:83
  25.6 8.0 %collective-permute-start.3 = (bf16[32,1536]{1,0:T(8,128)(2,1)S(1)}, bf16[32,1536]{1,0:T(8,128)(2,1)S(1)}, u32[]{:S(2)}, u32[]{:S(2)}) collective-permute-start(bf16[32,1536]{1,0:T(8,128)(2,1)S(1)} %get-tuple-element.15), channel_id=1, source_target_pairs={{528,0},{529,1},{530,2},{531,3},{532,4},{533,5},{534,6},{535,7},{5... | collective-permute-start | bytes 294920 | tf_op jit(solution)/shard_map/ppermute | solution.py:83
  33.7 7.1 %collective-permute-start.4 = (bf16[3,64,1536]{2,1,0:T(8,128)(2,1)S(1)}, bf16[3,64,1536]{2,1,0:T(8,128)(2,1)S(1)}, u32[]{:S(2)}, u32[]{:S(2)}) collective-permute-start(bf16[3,64,1536]{2,1,0:T(8,128)(2,1)S(1)} %pad_maximum_fusion), channel_id=1, source_target_pairs={{0,1},{1,0},{2,3},{3,2},{4,5},{5,4},{6,7},{7,6},{8,9},{9,8},{10,11... | collective-permute-start | bytes 1769480 | tf_op jit(solution)/shard_map/ppermute | solution.py:111
  41.9 42.8 %copy-start.5 = (bf16[1,1,2,64,64]{4,3,2,1,0:T(8,128)(2,1)S(1)}, bf16[1,1,2,64,64]{4,3,2,1,0:T(8,128)(2,1)}, u32[]{:S(2)}) copy-start(bf16[1,1,2,64,64]{4,3,2,1,0:T(8,128)(2,1)} %param.13) | copy-start | bytes 49156
  42.6 32.6 %all-to-all-start = ((f32[256,1,33]{2,1,0:T(1,128)}), f32[256,1,33]{2,1,0:T(1,128)S(1)}, u32[]{:S(2)}, u32[]{:S(2)}) async-start(f32[256,1,33]{2,1,0:T(1,128)} %bitcast.26), calls=%async_computation | async-start | bytes 262144 | tf_op jit(solution)/shard_map/all_to_all | solution.py:47
  76.9 24.8 %all-to-all-start.1 = ((bf16[256,1,32]{2,1,0:T(2,128)(2,1)}), bf16[256,1,32]{2,1,0:T(2,128)(2,1)S(1)}, u32[]{:S(2)}, u32[]{:S(2)}) async-start(bf16[256,1,32]{2,1,0:T(2,128)(2,1)} %convert), calls=%async_computation.1 | async-start | bytes 262144 | tf_op jit(solution)/shard_map/all_to_all | solution.py:59

commit v3 on v2

--- a/solution.py
+++ b/solution.py
@@ -36,27 +36,42 @@
     return state
 
 
-def entering_by_transpose(block_terms, block_total, axis):
-    size = lax.axis_size(axis)
+def gather_groups(message, outer):
+    return lax.all_to_all(jnp.broadcast_to(message, (outer,) + message.shape), "sx", 0, 0, tiled=True)
+
+
+def exact_weights(logs, start):
+    count = logs.shape[0]
+    rows = start.shape[0]
+    index = lax.broadcasted_iota(jnp.int32, (rows, count), 1)
+    later = index > start[:, None]
+    upper = lax.broadcasted_iota(jnp.int32, (count, count), 0) < lax.broadcasted_iota(
+        jnp.int32, (count, count), 1
+    )
+    chosen = jnp.where(later, logs[None, :], 0.0)
+    between = jnp.dot(chosen, upper.astype(jnp.float32), precision=lax.Precision.HIGHEST)
+    weights = jnp.where(later, jnp.exp(jnp.where(later, between, 0.0)), 0.0)
+    return weights, jnp.sum(chosen, axis=1)
+
+
+def entering_two_level(block_terms, block_total):
+    inner = lax.axis_size("sy")
     heads, rows, cols = block_terms.shape
-    piece = heads * rows * cols // size
-    owner_head = (jnp.arange(size) * piece) // (rows * cols)
+    piece = heads * rows * cols // inner
+    owner_head = (jnp.arange(inner) * piece) // (rows * cols)
     payload = jnp.concatenate(
-        [block_terms.reshape(size, piece), block_total[owner_head][:, None]], axis=1
-    )
-    gathered = lax.all_to_all(payload, axis, 0, 0, tiled=True)
-    totals = gathered[:, piece]
-    later = lax.broadcasted_iota(jnp.int32, (size, size), 1) > lax.broadcasted_iota(
-        jnp.int32, (size, size), 0
-    )
-    between = jnp.dot(
-        jnp.where(later, totals[None, :], 0.0),
-        later.astype(jnp.float32),
-        precision=lax.Precision.HIGHEST,
-    )
-    weights = jnp.where(later, jnp.exp(jnp.where(later, between, 0.0)), 0.0)
-    folded = jnp.dot(weights, gathered[:, :piece], precision=lax.Precision.HIGHEST)
-    returned = lax.all_to_all(folded, axis, 0, 0, tiled=True)
+        [block_terms.reshape(inner, piece), block_total[owner_head][:, None]], axis=1
+    )
+    got = lax.all_to_all(payload, "sy", 0, 0, tiled=True)
+    weights, tail_log = exact_weights(got[:, piece], jnp.arange(-1, inner))
+    folded = jnp.dot(weights, got[:, :piece], precision=lax.Precision.HIGHEST)
+    message = jnp.concatenate([folded[0], jnp.broadcast_to(tail_log[0], (128,))])
+    outer = lax.axis_size("sx")
+    groups = gather_groups(message, outer)
+    group_weights, _ = exact_weights(groups[:, piece], lax.axis_index("sx")[None])
+    incoming = jnp.dot(group_weights, groups[:, :piece], precision=lax.Precision.HIGHEST)
+    future = folded[1:] + jnp.exp(tail_log[1:])[:, None] * incoming
+    returned = lax.all_to_all(future, "sy", 0, 0, tiled=True)
     return returned.reshape(heads, rows, cols)
 
 
@@ -80,7 +95,7 @@
                 for core in range(CORES):
                     src = linear((z + distance) % z_size, x, y, core, z_lo_size)
                     pairs.append((src, linear(z, x, y, core, z_lo_size)))
-    return lax.ppermute(array, ("dp", "seq"), pairs)
+    return lax.ppermute(array, ("dp", "sx", "sy"), pairs)
 
 
 def partial_product(token_rows, block, index, cols):
@@ -91,7 +106,7 @@
 def project(token_rows, w_local):
     z_lo_size = lax.axis_size("dp")
     z_lo = lax.axis_index("dp")
-    core = lax.axis_index("seq") % CORES
+    core = lax.axis_index("sy") % CORES
     cols = w_local.shape[1]
     half = w_local.shape[0] // CORES
     quarter = half // 2
@@ -109,8 +124,8 @@
     fetched = [near_up, near_down, far]
     offsets = [1, z_lo_size - 1, 2]
     swapped = lax.ppermute(
-        jnp.stack(fetched), "seq",
-        [(i, i ^ 1) for i in range(lax.axis_size("seq"))],
+        jnp.stack(fetched), "sy",
+        [(i, i ^ 1) for i in range(lax.axis_size("sy"))],
     )
     own_mine = partial_product(token_rows, mine, z_lo, cols)
     own_theirs = partial_product(token_rows, theirs, z_lo, cols)
@@ -151,7 +166,7 @@
         ],
         axis=1,
     )
-    future = entering_by_transpose(block_terms, block_total, "seq")
+    future = entering_two_level(block_terms, block_total)
     future_low = future.astype(jnp.bfloat16)
     log_gaps = cumul[:, :, None] - cumul[:, None, :]
     rows_idx = lax.broadcasted_iota(jnp.int32, (length_dev, length_dev), 0)
@@ -189,18 +204,22 @@
 
 
 def solution(mesh):
+    inner = Y_SIZE * CORES
+    blocks = mesh.devices.reshape(mesh.shape["dp"], mesh.shape["seq"] // inner, inner)
+    grid = jax.sharding.Mesh(blocks, ("dp", "sx", "sy"))
+    seq = ("sx", "sy")
     return jax.shard_map(
         on_device,
-        mesh=mesh,
+        mesh=grid,
         in_specs=(
-            P("dp", "seq", None),
+            P("dp", seq, None),
             P(None, "dp"),
-            P("dp", "seq", None),
-            P("dp", "seq", None),
-            P("dp", "seq", None),
-            P("dp", None, "seq"),
-            P("dp", "seq", None, None, None),
+            P("dp", seq, None),
+            P("dp", seq, None),
+            P("dp", seq, None),
+            P("dp", None, seq),
+            P("dp", seq, None, None, None),
         ),
-        out_specs=(P("dp", "seq", None), P("dp", "seq", None), P("dp", "seq", None)),
+        out_specs=(P("dp", seq, None), P("dp", seq, None), P("dp", seq, None)),
         check_vma=False,
     )

time: 105 us -> 95.2 us (0.907)
  waiting for transfers between devices: 34.1 us -> 26.7 us
  starting transfers between devices: 55 us -> 51 us
  local copies, waits for them, and re-layouts: 6.14 us -> 8.45 us
    all_to_all x2 -> x3, waiting for transfers between devices: 32.7 us -> 25.2 us  [the longest x1 11.6 us: gather_groups(): lax.all_to_all(jnp.broadcast_to(message, (outer,) + message.shape), 'sx',...]
    all_to_all x2 -> x3, starting transfers between devices: 23.5 us -> 19.5 us  [the longest x1 7.94 us: entering_two_level(): got = lax.all_to_all(payload, 'sy', 0, 0, tiled=True)]
    all_to_all x0 -> x2, local copies, waits for them, and re-layouts: none -> 1.16 us  [the longest x1 0.64 us: entering_two_level(): got = lax.all_to_all(payload, 'sy', 0, 0, tiled=True)]
    unnamed x19 -> x23, local copies, waits for them, and re-layouts: 2.58 us -> 3.22 us
  transfers between devices with their start and end apart: 7 -> 8, of which waited for: 4 -> 5; matrix products, arithmetic and copies ran while one was open for 7% -> 7% of each run, Pallas kernels for 0% -> 0%
where the time goes in v3:
time: 95.2 us; the launch traced here: 94.7 us
  starting transfers between devices  51 us (54%)
  waiting for transfers between devices  26.7 us (28%)
  local copies, waits for them, and re-layouts  8.45 us (9%)
  matrix products  4.24 us (4%)
  other arithmetic  3.29 us (3%)
  between operations  1.06 us (1%)
    ppermute x4, starting transfers between devices, from_offset(): return lax.ppermute(array, ('dp', 'sx', 'sy'), pairs)  26 us
    all_to_all x1, waiting for transfers between devices, gather_groups(): lax.all_to_all(jnp.broadcast_to(message, (outer,) + message.shape), 'sx',...  11.6 us
    all_to_all x1, starting transfers between devices, entering_two_level(): got = lax.all_to_all(payload, 'sy', 0, 0, tiled=True)  7.94 us
    all_to_all x1, waiting for transfers between devices, entering_two_level(): got = lax.all_to_all(payload, 'sy', 0, 0, tiled=True)  7.05 us
    all_to_all x1, starting transfers between devices, gather_groups(): lax.all_to_all(jnp.broadcast_to(message, (outer,) + message.shape), 'sx',...  6.58 us
    all_to_all x1, waiting for transfers between devices, entering_two_level(): returned = lax.all_to_all(future, 'sy', 0, 0, tiled=True)  6.54 us
    ppermute x1, starting transfers between devices, project(): lax.ppermute(jnp.stack(fetched), 'sy', [(i, i ^ 1) for i in range(lax.axi...  5.48 us
    all_to_all x1, starting transfers between devices, entering_two_level(): returned = lax.all_to_all(future, 'sy', 0, 0, tiled=True)  5.01 us
  transfers between devices with their start and end apart: 8, of which 5 were waited for; matrix products, arithmetic and copies ran while one was open for 7% of the time, Pallas kernels for 0%

profile of v3, /device:TPU:1, one launch (start us, length us, event | category | flops | bytes accessed | tf_op | source)
XLA Modules:
  0.0 94.7 jit_solution(6029761279092545430)
XLA Ops:
  0.7 1.1 %constant_dynamic-slice_fusion.2 = bf16[64,1536]{1,0:T(8,128)(2,1)S(1)} fusion(bf16[128,1536]{1,0:T(8,128)(2,1)} %param.8, s32[]{:T(128)S(6)} %select_n.108), kind=kLoop, calls=%fused_computation.115 | loop fusion | bytes 393220 | tf_op jit(solution)/shard_map/dynamic_slice | solution.py:113
  1.8 17.9 %collective-permute-start = (bf16[64,1536]{1,0:T(8,128)(2,1)S(1)}, bf16[64,1536]{1,0:T(8,128)(2,1)S(1)}, u32[]{:S(2)}, u32[]{:S(2)}) collective-permute-start(bf16[64,1536]{1,0:T(8,128)(2,1)S(1)} %constant_dynamic-slice_fusion.2), channel_id=1, source_target_pairs={{256,0},{257,1},{258,2},{259,3},{260,4},{261,5},{262,6},{263,7},{2... | collective-permute-start | bytes 589832 | tf_op jit(solution)/shard_map/ppermute | solution.py:98
  19.7 1.9 %collective-permute-start.1 = (bf16[64,1536]{1,0:T(8,128)(2,1)S(1)}, bf16[64,1536]{1,0:T(8,128)(2,1)S(1)}, u32[]{:S(2)}, u32[]{:S(2)}) collective-permute-start(bf16[64,1536]{1,0:T(8,128)(2,1)S(1)} %constant_dynamic-slice_fusion.2), channel_id=1, source_target_pairs={{784,0},{785,1},{786,2},{787,3},{788,4},{789,5},{790,6},{791,7},{7... | collective-permute-start | bytes 589832 | tf_op jit(solution)/shard_map/ppermute | solution.py:98
  21.6 1.0 %constant_dynamic-slice_fusion = (bf16[32,1536]{1,0:T(8,128)(2,1)S(1)}, bf16[32,1536]{1,0:T(8,128)(2,1)S(1)}) fusion(bf16[128,1536]{1,0:T(8,128)(2,1)} %param.8, s32[]{:T(128)S(6)} %add.134, s32[]{:T(128)S(6)} %select_n.108), kind=kLoop, calls=%fused_computation.109 | loop fusion | bytes 393224 | tf_op jit(solution)/shard_map/slice | solution.py:120
  22.5 3.1 %collective-permute-start.2 = (bf16[32,1536]{1,0:T(8,128)(2,1)S(1)}, bf16[32,1536]{1,0:T(8,128)(2,1)S(1)}, u32[]{:S(2)}, u32[]{:S(2)}) collective-permute-start(bf16[32,1536]{1,0:T(8,128)(2,1)S(1)} %get-tuple-element.16), channel_id=1, source_target_pairs={{512,0},{513,1},{514,2},{515,3},{516,4},{517,5},{518,6},{519,7},{5... | collective-permute-start | bytes 294920 | tf_op jit(solution)/shard_map/ppermute | solution.py:98
  25.6 3.1 %collective-permute-start.3 = (bf16[32,1536]{1,0:T(8,128)(2,1)S(1)}, bf16[32,1536]{1,0:T(8,128)(2,1)S(1)}, u32[]{:S(2)}, u32[]{:S(2)}) collective-permute-start(bf16[32,1536]{1,0:T(8,128)(2,1)S(1)} %get-tuple-element.15), channel_id=1, source_target_pairs={{528,0},{529,1},{530,2},{531,3},{532,4},{533,5},{534,6},{535,7},{5... | collective-permute-start | bytes 294920 | tf_op jit(solution)/shard_map/ppermute | solution.py:98
  28.8 1.0 %reduce_window_sum.11 = f32[2,128]{1,0:T(2,128)S(1)} reduce-window(f32[2,128]{1,0:T(2,128)} %bitcast.146, f32[]{:T(128)} %constant.77.clone.1), window={size=1x128 pad=0_0x127_0}, to_apply=%region_0.1 | reduce-window | flops 32512 | bytes 2052 | tf_op jit(solution)/shard_map/jit(cumsum)/reduce_window_sum | solution.py:153
  29.8 0.2 slice_reduce_fusion.2
  30.0 0.6 fusion.81
  30.6 0.3 fusion.33
  30.9 0.3 fusion.31
  31.2 0.1 copy.38
  31.6 1.3 %fusion.61 = f32[16,1]{1,0:T(8,128)S(1)} fusion(f32[]{:T(128)} %bitcast.24, f32[]{:T(128)} %bitcast.23), kind=kLoop, calls=%fused_computation.99 | loop fusion | flops 336 | bytes 72 | tf_op jit(solution)/shard_map/gather | solution.py:63
  33.0 0.7 collective-permute-done.3
  33.7 5.5 %collective-permute-start.4 = (bf16[3,64,1536]{2,1,0:T(8,128)(2,1)S(1)}, bf16[3,64,1536]{2,1,0:T(8,128)(2,1)S(1)}, u32[]{:S(2)}, u32[]{:S(2)}) collective-permute-start(bf16[3,64,1536]{2,1,0:T(8,128)(2,1)S(1)} %pad_maximum_fusion), channel_id=1, source_target_pairs={{0,1},{1,0},{2,3},{3,2},{4,5},{5,4},{6,7},{7,6},{8,9},{9,8},{10,11... | collective-permute-start | bytes 1769480 | tf_op jit(solution)/shard_map/ppermute | solution.py:126
  39.2 0.3 fusion.25
  39.5 0.3 convolution_add_fusion.3
  39.8 0.3 fusion.14
  40.0 0.8 collective-permute-done.4
  40.8 0.2 fusion.23
  41.1 0.3 convolution_add_fusion.1
  41.4 0.3 fusion.16
  41.7 0.1 fusion.49
  41.9 0.6 all_to_all.20
  42.5 7.9 %all-to-all-start = ((f32[16,1,513]{2,1,0:T(1,128)}), f32[16,1,513]{2,1,0:T(1,128)S(1)}, u32[]{:S(2)}, u32[]{:S(2)}) async-start(f32[16,1,513]{2,1,0:T(1,128)} %all_to_all.20), calls=%async_computation | async-start | bytes 81920 | tf_op jit(solution)/shard_map/all_to_all | solution.py:65
  50.5 0.2 fusion
  50.7 0.1 convolution_bitcast_fusion.4
  50.8 7.1 %all-to-all-done = f32[16,1,513]{2,1,0:T(1,128)S(1)} async-done(((f32[16,1,513]{2,1,0:T(1,128)}), f32[16,1,513]{2,1,0:T(1,128)S(1)}, u32[]{:S(2)}, u32[]{:S(2)}) %all-to-all-start) | async-done | bytes 32864 | tf_op jit(solution)/shard_map/all_to_all | solution.py:65
  58.0 0.2 fusion.18
  58.3 0.2 fusion.53
  58.6 0.6 broadcast_in_dim.55
  59.3 6.6 %all-to-all-start.1 = ((f32[16,1,640]{2,1,0:T(1,128)}), f32[16,1,640]{2,1,0:T(1,128)S(1)}, u32[]{:S(2)}, u32[]{:S(2)}) async-start(f32[16,1,640]{2,1,0:T(1,128)} %broadcast_in_dim.55), calls=%async_computation.1 | async-start | bytes 81920 | tf_op jit(solution)/shard_map/all_to_all | solution.py:40
  65.9 11.6 %all-to-all-done.1 = f32[16,1,640]{2,1,0:T(1,128)S(1)} async-done(((f32[16,1,640]{2,1,0:T(1,128)}), f32[16,1,640]{2,1,0:T(1,128)S(1)}, u32[]{:S(2)}, u32[]{:S(2)}) %all-to-all-start.1) | async-done | bytes 40992 | tf_op jit(solution)/shard_map/all_to_all | solution.py:40
  77.7 0.1 fusion.22
  77.8 0.1 fusion.50
  78.0 0.5 broadcast.148
  78.5 0.7 reduce.8
  79.2 0.6 reshape.193
  79.8 5.0 %all-to-all-start.2 = ((bf16[16,2,256]{2,1,0:T(2,128)(2,1)}), bf16[16,2,256]{2,1,0:T(2,128)(2,1)S(1)}, u32[]{:S(2)}, u32[]{:S(2)}) async-start(bf16[16,2,256]{2,1,0:T(2,128)(2,1)} %reshape.193), calls=%async_computation.2 | async-start | bytes 32768 | tf_op jit(solution)/shard_map/all_to_all | solution.py:74
  84.8 0.1 fusion.10
  85.0 0.7 copy.41
  85.7 6.5 %all-to-all-done.2 = bf16[16,2,256]{2,1,0:T(2,128)(2,1)S(1)} async-done(((bf16[16,2,256]{2,1,0:T(2,128)(2,1)}), bf16[16,2,256]{2,1,0:T(2,128)(2,1)S(1)}, u32[]{:S(2)}, u32[]{:S(2)}) %all-to-all-start.2) | async-done | bytes 16416 | tf_op jit(solution)/shard_map/all_to_all | solution.py:74
  92.4 0.2 fusion.8
  92.6 0.1 fusion.9
  92.8 0.3 fusion.12
  93.1 0.7 copy.43
  93.8 0.1 fusion.11
  94.0 0.7 copy.42
  (37 shorter events, 1.3 us)
Async XLA Ops:
  0.6 29.9 %copy-start = (bf16[1,128,6144]{2,1,0:T(8,128)(2,1)S(1)}, bf16[1,128,6144]{2,1,0:T(8,128)(2,1)}, u32[]{:S(2)}) copy-start(bf16[1,128,6144]{2,1,0:T(8,128)(2,1)} %param.7) | copy-start | bytes 4718596
  0.6 30.2 %copy-start.1 = (bf16[128,1536]{1,0:T(8,128)(2,1)S(1)}, bf16[128,1536]{1,0:T(8,128)(2,1)}, u32[]{:S(2)}) copy-start(bf16[128,1536]{1,0:T(8,128)(2,1)} %param.8) | copy-start | bytes 1179652
  0.7 30.5 %copy-start.2 = (bf16[1,128,128]{2,1,0:T(8,128)(2,1)S(1)}, bf16[1,128,128]{2,1,0:T(8,128)(2,1)}, u32[]{:S(2)}) copy-start(bf16[1,128,128]{2,1,0:T(8,128)(2,1)} %param.9) | copy-start | bytes 98308
  0.7 30.7 %copy-start.3 = (bf16[1,128,128]{2,1,0:T(8,128)(2,1)S(1)}, bf16[1,128,128]{2,1,0:T(8,128)(2,1)}, u32[]{:S(2)}) copy-start(bf16[1,128,128]{2,1,0:T(8,128)(2,1)} %param.10) | copy-start | bytes 98308
  0.7 30.8 %copy-start.4 = (bf16[1,128,128]{2,1,0:T(8,128)(2,1)S(1)}, bf16[1,128,128]{2,1,0:T(8,128)(2,1)}, u32[]{:S(2)}) copy-start(bf16[1,128,128]{2,1,0:T(8,128)(2,1)} %param.11) | copy-start | bytes 98308
  1.8 31.9 %collective-permute-start = (bf16[64,1536]{1,0:T(8,128)(2,1)S(1)}, bf16[64,1536]{1,0:T(8,128)(2,1)S(1)}, u32[]{:S(2)}, u32[]{:S(2)}) collective-permute-start(bf16[64,1536]{1,0:T(8,128)(2,1)S(1)} %constant_dynamic-slice_fusion.2), channel_id=1, source_target_pairs={{256,0},{257,1},{258,2},{259,3},{260,4},{261,5},{262,6},{263,7},{2... | collective-permute-start | bytes 589832 | tf_op jit(solution)/shard_map/ppermute | solution.py:98
  19.7 14.0 %collective-permute-start.1 = (bf16[64,1536]{1,0:T(8,128)(2,1)S(1)}, bf16[64,1536]{1,0:T(8,128)(2,1)S(1)}, u32[]{:S(2)}, u32[]{:S(2)}) collective-permute-start(bf16[64,1536]{1,0:T(8,128)(2,1)S(1)} %constant_dynamic-slice_fusion.2), channel_id=1, source_target_pairs={{784,0},{785,1},{786,2},{787,3},{788,4},{789,5},{790,6},{791,7},{7... | collective-permute-start | bytes 589832 | tf_op jit(solution)/shard_map/ppermute | solution.py:98
  22.5 10.4 %collective-permute-start.2 = (bf16[32,1536]{1,0:T(8,128)(2,1)S(1)}, bf16[32,1536]{1,0:T(8,128)(2,1)S(1)}, u32[]{:S(2)}, u32[]{:S(2)}) collective-permute-start(bf16[32,1536]{1,0:T(8,128)(2,1)S(1)} %get-tuple-element.16), channel_id=1, source_target_pairs={{512,0},{513,1},{514,2},{515,3},{516,4},{517,5},{518,6},{519,7},{5... | collective-permute-start | bytes 294920 | tf_op jit(solution)/shard_map/ppermute | solution.py:98
  25.6 8.0 %collective-permute-start.3 = (bf16[32,1536]{1,0:T(8,128)(2,1)S(1)}, bf16[32,1536]{1,0:T(8,128)(2,1)S(1)}, u32[]{:S(2)}, u32[]{:S(2)}) collective-permute-start(bf16[32,1536]{1,0:T(8,128)(2,1)S(1)} %get-tuple-element.15), channel_id=1, source_target_pairs={{528,0},{529,1},{530,2},{531,3},{532,4},{533,5},{534,6},{535,7},{5... | collective-permute-start | bytes 294920 | tf_op jit(solution)/shard_map/ppermute | solution.py:98
  33.7 7.1 %collective-permute-start.4 = (bf16[3,64,1536]{2,1,0:T(8,128)(2,1)S(1)}, bf16[3,64,1536]{2,1,0:T(8,128)(2,1)S(1)}, u32[]{:S(2)}, u32[]{:S(2)}) collective-permute-start(bf16[3,64,1536]{2,1,0:T(8,128)(2,1)S(1)} %pad_maximum_fusion), channel_id=1, source_target_pairs={{0,1},{1,0},{2,3},{3,2},{4,5},{5,4},{6,7},{7,6},{8,9},{9,8},{10,11... | collective-permute-start | bytes 1769480 | tf_op jit(solution)/shard_map/ppermute | solution.py:126
  41.1 43.7 %copy-start.5 = (bf16[1,1,2,64,64]{4,3,2,1,0:T(8,128)(2,1)S(1)}, bf16[1,1,2,64,64]{4,3,2,1,0:T(8,128)(2,1)}, u32[]{:S(2)}) copy-start(bf16[1,1,2,64,64]{4,3,2,1,0:T(8,128)(2,1)} %param.13) | copy-start | bytes 49156
  42.5 15.4 %all-to-all-start = ((f32[16,1,513]{2,1,0:T(1,128)}), f32[16,1,513]{2,1,0:T(1,128)S(1)}, u32[]{:S(2)}, u32[]{:S(2)}) async-start(f32[16,1,513]{2,1,0:T(1,128)} %all_to_all.20), calls=%async_computation | async-start | bytes 81920 | tf_op jit(solution)/shard_map/all_to_all | solution.py:65
  59.3 18.3 %all-to-all-start.1 = ((f32[16,1,640]{2,1,0:T(1,128)}), f32[16,1,640]{2,1,0:T(1,128)S(1)}, u32[]{:S(2)}, u32[]{:S(2)}) async-start(f32[16,1,640]{2,1,0:T(1,128)} %broadcast_in_dim.55), calls=%async_computation.1 | async-start | bytes 81920 | tf_op jit(solution)/shard_map/all_to_all | solution.py:40
  79.8 12.4 %all-to-all-start.2 = ((bf16[16,2,256]{2,1,0:T(2,128)(2,1)}), bf16[16,2,256]{2,1,0:T(2,128)(2,1)S(1)}, u32[]{:S(2)}, u32[]{:S(2)}) async-start(bf16[16,2,256]{2,1,0:T(2,128)(2,1)} %reshape.193), calls=%async_computation.2 | async-start | bytes 32768 | tf_op jit(solution)/shard_map/all_to_all | solution.py:74

commit v4 on v3

--- a/solution.py
+++ b/solution.py
@@ -36,10 +36,6 @@
     return state
 
 
-def gather_groups(message, outer):
-    return lax.all_to_all(jnp.broadcast_to(message, (outer,) + message.shape), "sx", 0, 0, tiled=True)
-
-
 def exact_weights(logs, start):
     count = logs.shape[0]
     rows = start.shape[0]
@@ -54,24 +50,44 @@
     return weights, jnp.sum(chosen, axis=1)
 
 
+def tiles(rows, scalar, height):
+    count = rows.shape[0]
+    body = rows.reshape(count, -1, 128)
+    spare = height - body.shape[1] - 1
+    return jnp.concatenate(
+        [
+            body,
+            jnp.broadcast_to(scalar[:, None, None], (count, 1, 128)),
+            jnp.zeros((count, spare, 128), rows.dtype),
+        ],
+        axis=1,
+    )
+
+
 def entering_two_level(block_terms, block_total):
     inner = lax.axis_size("sy")
     heads, rows, cols = block_terms.shape
     piece = heads * rows * cols // inner
+    height = piece // 128 + 1
+    height = -(-height // 8) * 8
     owner_head = (jnp.arange(inner) * piece) // (rows * cols)
-    payload = jnp.concatenate(
-        [block_terms.reshape(inner, piece), block_total[owner_head][:, None]], axis=1
-    )
+    payload = tiles(block_terms.reshape(inner, piece), block_total[owner_head], height)
     got = lax.all_to_all(payload, "sy", 0, 0, tiled=True)
-    weights, tail_log = exact_weights(got[:, piece], jnp.arange(-1, inner))
-    folded = jnp.dot(weights, got[:, :piece], precision=lax.Precision.HIGHEST)
-    message = jnp.concatenate([folded[0], jnp.broadcast_to(tail_log[0], (128,))])
+    weights, tail_log = exact_weights(got[:, piece // 128, 0], jnp.arange(-1, inner))
+    terms = got[:, : piece // 128].reshape(inner, piece)
+    folded = jnp.dot(weights, terms, precision=lax.Precision.HIGHEST)
     outer = lax.axis_size("sx")
-    groups = gather_groups(message, outer)
-    group_weights, _ = exact_weights(groups[:, piece], lax.axis_index("sx")[None])
-    incoming = jnp.dot(group_weights, groups[:, :piece], precision=lax.Precision.HIGHEST)
+    message = tiles(folded[:1], tail_log[:1], height)
+    groups = lax.all_to_all(
+        jnp.broadcast_to(message, (outer,) + message.shape[1:]), "sx", 0, 0, tiled=True
+    )
+    group_weights, _ = exact_weights(groups[:, piece // 128, 0], lax.axis_index("sx")[None])
+    incoming = jnp.dot(
+        group_weights, groups[:, : piece // 128].reshape(outer, piece),
+        precision=lax.Precision.HIGHEST,
+    )
     future = folded[1:] + jnp.exp(tail_log[1:])[:, None] * incoming
-    returned = lax.all_to_all(future, "sy", 0, 0, tiled=True)
+    returned = lax.all_to_all(future.reshape(inner, -1, 128), "sy", 0, 0, tiled=True)
     return returned.reshape(heads, rows, cols)
 
 
@@ -86,14 +102,14 @@
     return (z % z_lo_size) * (X_SIZE * Z_HI * Y_SIZE * CORES) + seq
 
 
-def from_offset(array, distance, z_lo_size):
+def from_offset(array, distances, z_lo_size):
     z_size = z_lo_size * Z_HI
     pairs = []
     for z in range(z_size):
         for x in range(X_SIZE):
             for y in range(Y_SIZE):
                 for core in range(CORES):
-                    src = linear((z + distance) % z_size, x, y, core, z_lo_size)
+                    src = linear((z + distances[core]) % z_size, x, y, core, z_lo_size)
                     pairs.append((src, linear(z, x, y, core, z_lo_size)))
     return lax.ppermute(array, ("dp", "sx", "sy"), pairs)
 
@@ -109,34 +125,25 @@
     core = lax.axis_index("sy") % CORES
     cols = w_local.shape[1]
     half = w_local.shape[0] // CORES
-    quarter = half // 2
-    mine = lax.dynamic_slice_in_dim(w_local, core * half, half, 0)
-    theirs = lax.dynamic_slice_in_dim(w_local, (1 - core) * half, half, 0)
-    near_up = from_offset(mine, 1, z_lo_size)
-    near_down = from_offset(mine, -1, z_lo_size)
-    far = jnp.concatenate(
-        [
-            from_offset(mine[:quarter], 2, z_lo_size),
-            from_offset(mine[quarter:], -2, z_lo_size),
-        ],
-        axis=0,
-    )
-    fetched = [near_up, near_down, far]
-    offsets = [1, z_lo_size - 1, 2]
+    near = from_offset(w_local, (1, -1), z_lo_size)
+    far = from_offset(lax.dynamic_slice_in_dim(w_local, core * half, half, 0), (2, -2), z_lo_size)
     swapped = lax.ppermute(
-        jnp.stack(fetched), "sy",
+        jnp.concatenate([near, far], axis=0), "sy",
         [(i, i ^ 1) for i in range(lax.axis_size("sy"))],
     )
-    own_mine = partial_product(token_rows, mine, z_lo, cols)
-    own_theirs = partial_product(token_rows, theirs, z_lo, cols)
-    for k in range(3):
-        index = (z_lo + offsets[k]) % z_lo_size
-        own_mine = own_mine + partial_product(token_rows, fetched[k], index, cols)
-        own_theirs = own_theirs + partial_product(token_rows, swapped[k], index, cols)
-    return jnp.where(
+    step = 1 - 2 * core
+    total = partial_product(token_rows, w_local, z_lo, cols)
+    total = total + partial_product(token_rows, near, (z_lo + step) % z_lo_size, cols)
+    total = total + partial_product(
+        token_rows, swapped[: w_local.shape[0]], (z_lo - step) % z_lo_size, cols
+    )
+    far_index = (z_lo + 2) % z_lo_size
+    far_mine = partial_product(token_rows, far, far_index, cols)
+    far_theirs = partial_product(token_rows, swapped[w_local.shape[0]:], far_index, cols)
+    return total + jnp.where(
         core == 0,
-        jnp.concatenate([own_mine, own_theirs], axis=1),
-        jnp.concatenate([own_theirs, own_mine], axis=1),
+        jnp.concatenate([far_mine, far_theirs], axis=1),
+        jnp.concatenate([far_theirs, far_mine], axis=1),
     )
 
 

time: 95.2 us -> 88.5 us (0.930)
  starting transfers between devices: 51 us -> 35.9 us
  waiting for transfers between devices: 26.7 us -> 36.3 us
  local copies, waits for them, and re-layouts: 8.45 us -> 6.5 us
    ppermute x4 -> x2, starting transfers between devices: 26 us -> 13.5 us  [from_offset(): return lax.ppermute(array, ('dp', 'sx', 'sy'), pairs)]
    ppermute x4 -> x2, waiting for transfers between devices: 0.68 us -> 10.6 us  [from_offset(): return lax.ppermute(array, ('dp', 'sx', 'sy'), pairs)]
    ppermute x1, starting transfers between devices: 5.48 us -> 2.57 us  [project(): lax.ppermute(jnp.concatenate([near, far], axis=0), 'sy', [(i, i ^ 1) for...]
    all_to_all x2 -> x0, local copies, waits for them, and re-layouts: 1.16 us -> none  [the longest x1 0.64 us: entering_two_level(): got = lax.all_to_all(payload, 'sy', 0, 0, tiled=True)]
    unnamed x23 -> x18, local copies, waits for them, and re-layouts: 3.22 us -> 2.56 us
    dot_general x8 -> x5, matrix products: 2.09 us -> 2.33 us  [partial_product(): lax.dot_general(rows, block, (((1,), (1,)), ((), ())), preferred_element_...]
  transfers between devices with their start and end apart: 8 -> 6, of which waited for: 5 -> 4; matrix products, arithmetic and copies ran while one was open for 7% -> 9% of each run, Pallas kernels for 0% -> 0%
where the time goes in v4:
time: 88.5 us; the launch traced here: 88 us
  waiting for transfers between devices  36.3 us (41%)
  starting transfers between devices  35.9 us (41%)
  local copies, waits for them, and re-layouts  6.5 us (7%)
  matrix products  4.44 us (5%)
  other arithmetic  3.87 us (4%)
  between operations  1 us (1%)
    ppermute x2, starting transfers between devices, from_offset(): return lax.ppermute(array, ('dp', 'sx', 'sy'), pairs)  13.5 us
    all_to_all x1, waiting for transfers between devices, entering_two_level(): lax.all_to_all(jnp.broadcast_to(message, (outer,) + message.shape[1:]), '...  11.7 us
    ppermute x2, waiting for transfers between devices, from_offset(): return lax.ppermute(array, ('dp', 'sx', 'sy'), pairs)  10.6 us
    all_to_all x1, starting transfers between devices, entering_two_level(): lax.all_to_all(jnp.broadcast_to(message, (outer,) + message.shape[1:]), '...  7.49 us
    all_to_all x1, waiting for transfers between devices, entering_two_level(): got = lax.all_to_all(payload, 'sy', 0, 0, tiled=True)  7.45 us
    all_to_all x1, starting transfers between devices, entering_two_level(): got = lax.all_to_all(payload, 'sy', 0, 0, tiled=True)  7.41 us
    all_to_all x1, waiting for transfers between devices, entering_two_level(): lax.all_to_all(future.reshape(inner, -1, 128), 'sy', 0, 0, tiled=True)  6.55 us
    all_to_all x1, starting transfers between devices, entering_two_level(): lax.all_to_all(future.reshape(inner, -1, 128), 'sy', 0, 0, tiled=True)  4.87 us
  transfers between devices with their start and end apart: 6, of which 4 were waited for; matrix products, arithmetic and copies ran while one was open for 9% of the time, Pallas kernels for 0%

profile of v4, /device:TPU:1, one launch (start us, length us, event | category | flops | bytes accessed | tf_op | source)
XLA Modules:
  0.0 88.0 jit_solution(13313911324989356248)
XLA Ops:
  0.7 5.9 %collective-permute-start = (bf16[128,1536]{1,0:T(8,128)(2,1)}, bf16[128,1536]{1,0:T(8,128)(2,1)S(1)}, u32[]{:S(2)}, u32[]{:S(2)}) collective-permute-start(bf16[128,1536]{1,0:T(8,128)(2,1)} %param.8), channel_id=1, source_target_pairs={{256,0},{785,1},{258,2},{787,3},{260,4},{789,5},{262,6},{791,7},{2... | collective-permute-start | bytes 1179656 | tf_op jit(solution)/shard_map/ppermute | solution.py:114
  6.6 1.0 %constant_dynamic-slice_fusion = bf16[64,1536]{1,0:T(8,128)(2,1)S(1)} fusion(bf16[128,1536]{1,0:T(8,128)(2,1)} %param.8, s32[]{:T(128)S(6)} %select_n.104), kind=kLoop, calls=%fused_computation.82 | loop fusion | bytes 393220 | tf_op jit(solution)/shard_map/dynamic_slice | solution.py:129
  7.5 7.6 %collective-permute-start.1 = (bf16[64,1536]{1,0:T(8,128)(2,1)S(1)}, bf16[64,1536]{1,0:T(8,128)(2,1)S(1)}, u32[]{:S(2)}, u32[]{:S(2)}) collective-permute-start(bf16[64,1536]{1,0:T(8,128)(2,1)S(1)} %constant_dynamic-slice_fusion), channel_id=1, source_target_pairs={{512,0},{529,1},{514,2},{531,3},{516,4},{533,5},{518,6},{535,7},{5... | collective-permute-start | bytes 589832 | tf_op jit(solution)/shard_map/ppermute | solution.py:114
  15.2 1.0 %reduce_window_sum.11 = f32[2,128]{1,0:T(2,128)S(1)} reduce-window(f32[2,128]{1,0:T(2,128)} %bitcast.131, f32[]{:T(128)} %constant.78.clone.1), window={size=1x128 pad=0_0x127_0}, to_apply=%region_0.1 | reduce-window | flops 32512 | bytes 2052 | tf_op jit(solution)/shard_map/jit(cumsum)/reduce_window_sum | solution.py:160
  16.2 0.2 slice_reduce_fusion.2
  16.4 1.3 %fusion.28 = f32[128,128]{0,1:T(8,128)S(1)} fusion(bf16[128,1536]{1,0:T(8,128)(2,1)} %param.8, bf16[1,128,6144]{2,1,0:T(8,128)(2,1)S(1)} %copy-done, s32[]{:T(128)S(6)} %select_n.98), kind=kOutput, calls=%fused_computation.40 | convolution fusion | flops 50331648 | bytes 851972 | tf_op jit(solution)/shard_map/dot_general | solution.py:119
  17.6 0.5 iota_add_fusion
  18.2 0.6 fusion.66
  18.8 10.6 %collective-permute-done.1 = bf16[64,1536]{1,0:T(8,128)(2,1)S(1)} collective-permute-done((bf16[64,1536]{1,0:T(8,128)(2,1)S(1)}, bf16[64,1536]{1,0:T(8,128)(2,1)S(1)}, u32[]{:S(2)}, u32[]{:S(2)}) %collective-permute-start.1) | collective-permute-done | bytes 196640 | tf_op jit(solution)/shard_map/ppermute | solution.py:114
  29.5 2.6 %collective-permute-start.2 = (bf16[192,1536]{1,0:T(8,128)(2,1)S(1)}, bf16[192,1536]{1,0:T(8,128)(2,1)S(1)}, u32[]{:S(2)}, u32[]{:S(2)}) collective-permute-start(bf16[192,1536]{1,0:T(8,128)(2,1)S(1)} %pad_maximum_fusion), channel_id=1, source_target_pairs={{0,1},{1,0},{2,3},{3,2},{4,5},{5,4},{6,7},{7,6},{8,9},{9,8},{10,11... | collective-permute-start | bytes 1769480 | tf_op jit(solution)/shard_map/ppermute | solution.py:130
  32.1 1.3 %fusion.60 = f32[16]{0:T(128)S(1)} fusion(f32[]{:T(128)} %bitcast.17, f32[]{:T(128)} %bitcast.16), kind=kLoop, calls=%fused_computation.94 | loop fusion | flops 336 | bytes 72 | tf_op jit(solution)/shard_map/gather | solution.py:74
  33.4 0.1 copy.37
  33.6 0.1 copy.36
  33.7 0.1 copy.35
  33.9 0.3 fusion.24
  34.2 0.3 convolution_add_fusion.1
  34.5 0.3 fusion.22
  34.8 0.3 fusion.11
  35.1 0.1 fusion.40
  35.2 0.1 reshape_reshape.3
  35.4 0.7 maximum_maximum_fusion
  36.1 7.4 %all-to-all-start = ((f32[16,8,128]{2,1,0:T(8,128)}), f32[16,8,128]{2,1,0:T(8,128)S(1)}, u32[]{:S(2)}, u32[]{:S(2)}) async-start(f32[16,8,128]{2,1,0:T(8,128)} %maximum_maximum_fusion), calls=%async_computation | async-start | bytes 131072 | tf_op jit(solution)/shard_map/all_to_all | solution.py:75
  43.5 0.2 fusion
  43.7 0.1 convolution_bitcast_fusion.4
  43.8 7.4 %all-to-all-done = f32[16,8,128]{2,1,0:T(8,128)S(1)} async-done(((f32[16,8,128]{2,1,0:T(8,128)}), f32[16,8,128]{2,1,0:T(8,128)S(1)}, u32[]{:S(2)}, u32[]{:S(2)}) %all-to-all-start) | async-done | bytes 65568 | tf_op jit(solution)/shard_map/all_to_all | solution.py:75
  51.3 0.2 slice_reduce_fusion.1
  51.5 0.1 select_reduce_fusion
  51.6 0.2 fusion.16
  51.8 0.1 pad.1.clone
  51.9 0.2 fusion.44
  52.2 0.6 broadcast_in_dim.80
  52.9 7.5 %all-to-all-start.1 = ((f32[16,8,128]{2,1,0:T(8,128)}), f32[16,8,128]{2,1,0:T(8,128)S(1)}, u32[]{:S(2)}, u32[]{:S(2)}) async-start(f32[16,8,128]{2,1,0:T(8,128)} %broadcast_in_dim.80), calls=%async_computation.1 | async-start | bytes 131072 | tf_op jit(solution)/shard_map/all_to_all | solution.py:81
  60.4 11.7 %all-to-all-done.1 = f32[16,8,128]{2,1,0:T(8,128)S(1)} async-done(((f32[16,8,128]{2,1,0:T(8,128)}), f32[16,8,128]{2,1,0:T(8,128)S(1)}, u32[]{:S(2)}, u32[]{:S(2)}) %all-to-all-start.1) | async-done | bytes 65568 | tf_op jit(solution)/shard_map/all_to_all | solution.py:81
  72.2 0.2 slice_reduce_fusion
  72.4 0.1 fusion.20
  72.5 0.1 fusion.41
  72.6 0.1 slice_add_fusion
  72.7 0.6 reshape.169
  73.4 4.9 %all-to-all-start.2 = ((bf16[16,4,128]{2,1,0:T(4,128)(2,1)}), bf16[16,4,128]{2,1,0:T(4,128)(2,1)S(1)}, u32[]{:S(2)}, u32[]{:S(2)}) async-start(bf16[16,4,128]{2,1,0:T(4,128)(2,1)} %reshape.169), calls=%async_computation.2 | async-start | bytes 32768 | tf_op jit(solution)/shard_map/all_to_all | solution.py:90
  78.2 0.1 fusion.12
  78.4 0.7 copy.39
  79.1 6.5 %all-to-all-done.2 = bf16[16,4,128]{2,1,0:T(4,128)(2,1)S(1)} async-done(((bf16[16,4,128]{2,1,0:T(4,128)(2,1)}), bf16[16,4,128]{2,1,0:T(4,128)(2,1)S(1)}, u32[]{:S(2)}, u32[]{:S(2)}) %all-to-all-start.2) | async-done | bytes 16416 | tf_op jit(solution)/shard_map/all_to_all | solution.py:90
  85.7 0.1 fusion.9
  85.9 0.2 fusion.8
  86.1 0.1 fusion.13
  86.2 0.7 copy.40
  86.9 0.3 fusion.14
  87.3 0.7 copy.41
  (26 shorter events, 0.6 us)
Async XLA Ops:
  0.6 15.7 %copy-start = (bf16[1,128,6144]{2,1,0:T(8,128)(2,1)S(1)}, bf16[1,128,6144]{2,1,0:T(8,128)(2,1)}, u32[]{:S(2)}) copy-start(bf16[1,128,6144]{2,1,0:T(8,128)(2,1)} %param.7) | copy-start | bytes 4718596
  0.6 32.8 %copy-start.2 = (bf16[1,128,128]{2,1,0:T(8,128)(2,1)S(1)}, bf16[1,128,128]{2,1,0:T(8,128)(2,1)}, u32[]{:S(2)}) copy-start(bf16[1,128,128]{2,1,0:T(8,128)(2,1)} %param.9) | copy-start | bytes 98308
  0.7 32.9 %copy-start.3 = (bf16[1,128,128]{2,1,0:T(8,128)(2,1)S(1)}, bf16[1,128,128]{2,1,0:T(8,128)(2,1)}, u32[]{:S(2)}) copy-start(bf16[1,128,128]{2,1,0:T(8,128)(2,1)} %param.10) | copy-start | bytes 98308
  0.7 33.0 %copy-start.4 = (bf16[1,128,128]{2,1,0:T(8,128)(2,1)S(1)}, bf16[1,128,128]{2,1,0:T(8,128)(2,1)}, u32[]{:S(2)}) copy-start(bf16[1,128,128]{2,1,0:T(8,128)(2,1)} %param.11) | copy-start | bytes 98308
  0.7 28.8 %collective-permute-start = (bf16[128,1536]{1,0:T(8,128)(2,1)}, bf16[128,1536]{1,0:T(8,128)(2,1)S(1)}, u32[]{:S(2)}, u32[]{:S(2)}) collective-permute-start(bf16[128,1536]{1,0:T(8,128)(2,1)} %param.8), channel_id=1, source_target_pairs={{256,0},{785,1},{258,2},{787,3},{260,4},{789,5},{262,6},{791,7},{2... | collective-permute-start | bytes 1179656 | tf_op jit(solution)/shard_map/ppermute | solution.py:114
  7.5 21.9 %collective-permute-start.1 = (bf16[64,1536]{1,0:T(8,128)(2,1)S(1)}, bf16[64,1536]{1,0:T(8,128)(2,1)S(1)}, u32[]{:S(2)}, u32[]{:S(2)}) collective-permute-start(bf16[64,1536]{1,0:T(8,128)(2,1)S(1)} %constant_dynamic-slice_fusion), channel_id=1, source_target_pairs={{512,0},{529,1},{514,2},{531,3},{516,4},{533,5},{518,6},{535,7},{5... | collective-permute-start | bytes 589832 | tf_op jit(solution)/shard_map/ppermute | solution.py:114
  29.5 5.0 %collective-permute-start.2 = (bf16[192,1536]{1,0:T(8,128)(2,1)S(1)}, bf16[192,1536]{1,0:T(8,128)(2,1)S(1)}, u32[]{:S(2)}, u32[]{:S(2)}) collective-permute-start(bf16[192,1536]{1,0:T(8,128)(2,1)S(1)} %pad_maximum_fusion), channel_id=1, source_target_pairs={{0,1},{1,0},{2,3},{3,2},{4,5},{5,4},{6,7},{7,6},{8,9},{9,8},{10,11... | collective-permute-start | bytes 1769480 | tf_op jit(solution)/shard_map/ppermute | solution.py:130
  34.2 17.3 %copy-start.5 = (s32[17]{0:T(128)S(1)}, s32[17]{0:T(128)}, u32[]{:S(2)}) copy-start(s32[17]{0:T(128)} %iota_add_fusion) | copy-start | bytes 208
  34.5 43.7 %copy-start.1 = (bf16[1,1,2,64,64]{4,3,2,1,0:T(8,128)(2,1)S(1)}, bf16[1,1,2,64,64]{4,3,2,1,0:T(8,128)(2,1)}, u32[]{:S(2)}) copy-start(bf16[1,1,2,64,64]{4,3,2,1,0:T(8,128)(2,1)} %param.13) | copy-start | bytes 49156
  36.1 15.2 %all-to-all-start = ((f32[16,8,128]{2,1,0:T(8,128)}), f32[16,8,128]{2,1,0:T(8,128)S(1)}, u32[]{:S(2)}, u32[]{:S(2)}) async-start(f32[16,8,128]{2,1,0:T(8,128)} %maximum_maximum_fusion), calls=%async_computation | async-start | bytes 131072 | tf_op jit(solution)/shard_map/all_to_all | solution.py:75
  52.9 19.3 %all-to-all-start.1 = ((f32[16,8,128]{2,1,0:T(8,128)}), f32[16,8,128]{2,1,0:T(8,128)S(1)}, u32[]{:S(2)}, u32[]{:S(2)}) async-start(f32[16,8,128]{2,1,0:T(8,128)} %broadcast_in_dim.80), calls=%async_computation.1 | async-start | bytes 131072 | tf_op jit(solution)/shard_map/all_to_all | solution.py:81
  73.4 12.3 %all-to-all-start.2 = ((bf16[16,4,128]{2,1,0:T(4,128)(2,1)}), bf16[16,4,128]{2,1,0:T(4,128)(2,1)S(1)}, u32[]{:S(2)}, u32[]{:S(2)}) async-start(bf16[16,4,128]{2,1,0:T(4,128)(2,1)} %reshape.169), calls=%async_computation.2 | async-start | bytes 32768 | tf_op jit(solution)/shard_map/all_to_all | solution.py:90
